TPU v7x, 512 devices: a whole 4x4x16 slice. The times are simulated.
512 devices in a mesh: pix: 64 (over z, x), tm: 8 (over y, core).
Axes of the slice: x: 4, y: 4, z: 16, core: 2. Of those that a mesh axis runs over, the one named last changes fastest.
Arguments:
- movie: bfloat16 [131072, 2048], P('pix', 'tm'), may hold values from -6 to 6
- traces: bfloat16 [2048, 2048], P('pix', 'tm'), may hold values from 0 to 2
- footprints: bfloat16 [16384, 128], P('pix'), may hold values from 0 to 0.2
- slot_block: int32 [16384], P('pix'), may hold values from 0 to 15
- slot_neuron: int32 [16384], P('pix'), may hold values from 0 to 31
- bucket_fill: int32 [64, 64], P('pix'), may hold values from 1 to 4, as said below
Outputs:
- traces_new: bfloat16 [2048, 2048], P('pix', 'tm')
- footprints_new: float32 [16384, 128], P('pix')
Inputs may be any that keep to these rules, and one draw needn't show every extreme that they name: `bucket_fill`: A tile has at most 4 used slots for one owner; in every draw some owner gets 4 from every tile, and every tile fills 4 for some owner.
All inputs are finite; a program needn't handle non-finite values.
Results may differ from a plain program's by a relative error of at most 0.0049.
Values may be sent and summed in bfloat16 or wider, within the bound.
No kernel may reach another device: no remote copies, remote signals or barrier semaphores. Data moves between devices by JAX's collectives and lax.ppermute only.
A program may use at most 64 MiB of HBM per device.

v0:
```python
import jax
import jax.numpy as jnp
from jax import lax
from jax.sharding import PartitionSpec as P

BLOCK = 128


def local(movie, traces, footprints, slot_block, slot_neuron, bucket_fill):
    pix_count = lax.axis_size("pix")
    slot_total = footprints.shape[0]
    capacity = slot_total // pix_count
    neur_local = traces.shape[0]
    block_count = movie.shape[0] // BLOCK
    slot_index = jnp.arange(slot_total, dtype=jnp.int32)
    bucket_of = slot_index // capacity
    position = slot_index % capacity
    owner_match = bucket_of[:, None] == jnp.arange(pix_count, dtype=jnp.int32)[None, :]
    fill_slot = jnp.sum(jnp.where(owner_match, bucket_fill[0][None, :], 0), axis=1)
    usable = position < fill_slot
    masked = footprints * usable[:, None].astype(jnp.bfloat16)
    block_pick = slot_block[:, None] == jnp.arange(block_count, dtype=jnp.int32)[None, :]
    dense_map = (block_pick.astype(jnp.bfloat16)[:, :, None] * masked[:, None, :]).reshape(
        slot_total, block_count * BLOCK
    )
    asked_ids = lax.all_to_all(
        slot_neuron.reshape(pix_count, capacity), "pix", split_axis=0, concat_axis=0, tiled=True
    )
    asked_flat = asked_ids.reshape(slot_total)

    def slot_rows(source_rows):
        gathered = lax.all_gather(source_rows, "pix", axis=0, tiled=True)
        global_row = bucket_of * neur_local + slot_neuron
        return gathered[global_row]

    def residual_of(slot_traces):
        rebuilt = lax.dot_general(
            dense_map, slot_traces, (((0,), (0,)), ((), ())), preferred_element_type=jnp.float32
        )
        return (movie.astype(jnp.float32) - rebuilt).astype(jnp.bfloat16)

    slot_traces = slot_rows(traces)
    residual = residual_of(slot_traces)
    projection = jnp.dot(dense_map, residual, preferred_element_type=jnp.float32)
    slot_power = jnp.sum(masked.astype(jnp.float32) ** 2, axis=1)
    got_proj, got_power = (
        lax.all_to_all(
            projection.reshape(pix_count, capacity, projection.shape[1]),
            "pix",
            split_axis=0,
            concat_axis=0,
            tiled=True,
        ),
        lax.all_to_all(
            slot_power.reshape(pix_count, capacity), "pix", split_axis=0, concat_axis=0, tiled=True
        ),
    )
    owner_pick = (jnp.arange(neur_local, dtype=jnp.int32)[:, None] == asked_flat[None, :]).astype(
        jnp.float32
    )
    summed = jnp.dot(
        owner_pick,
        got_proj.reshape(slot_total, projection.shape[1]),
        precision=lax.Precision.HIGHEST,
    )
    power = jnp.dot(owner_pick, got_power.reshape(slot_total), precision=lax.Precision.HIGHEST)
    updated = jnp.maximum(
        0.0, traces.astype(jnp.float32) + summed / jnp.maximum(power, 0.5)[:, None]
    ).astype(jnp.bfloat16)
    slot_updated = slot_rows(updated)
    residual_two = residual_of(slot_updated)
    products = lax.dot_general(
        residual_two, slot_updated, (((1,), (1,)), ((), ())), preferred_element_type=jnp.float32
    )
    numerator = jnp.einsum(
        "bps,sb->sp",
        products.reshape(block_count, BLOCK, slot_total),
        block_pick.astype(jnp.float32),
        precision=lax.Precision.HIGHEST,
    )
    trace_power = jnp.sum(slot_updated.astype(jnp.float32) ** 2, axis=1)
    numer_all, power_all = lax.psum((numerator, trace_power), "tm")
    grown = jnp.maximum(0.0, masked.astype(jnp.float32) + numer_all / (power_all + 1e-06)[:, None])
    return (updated, jnp.where(usable[:, None], grown, 0.0))


def solution(mesh):
    return jax.shard_map(
        local,
        mesh=mesh,
        in_specs=(
            P("pix", "tm"),
            P("pix", "tm"),
            P("pix", None),
            P("pix"),
            P("pix"),
            P("pix", None),
        ),
        out_specs=(P("pix", "tm"), P("pix", None)),
        check_vma=False,
    )
```

profile of v0, /device:TPU:1, one launch (start us, length us, event | category | flops | bytes accessed | tf_op | source)
XLA Modules:
  0.0 436.8 jit_solution(8261402427538340543)
XLA Ops:
  7.9 1.4 all_to_all.15
  9.3 19.1 %all-to-all-start = ((s32[64,1,4]{2,1,0:T(1,128)}), s32[64,1,4]{2,1,0:T(1,128)S(1)}, u32[]{:S(2)}, u32[]{:S(2)}) async-start(s32[64,1,4]{2,1,0:T(1,128)} %bitcast), calls=%async_computation | async-start | bytes 65536 | tf_op jit(solution)/shard_map/all_to_all | solution.py:26
  28.4 0.7 select_reduce_fusion
  29.8 0.8 fusion.24
  30.6 1.0 fusion.21
  33.4 112.6 %all-gather.3.cloned.1.call-done = bf16[2048,256]{1,0:T(8,128)(2,1)} async-done(((bf16[32,256]{1,0:T(8,128)(2,1)}), bf16[2048,256]{1,0:T(8,128)(2,1)}) %all-gather.3.cloned.1.call-update) | async-done | bytes 1048592 | tf_op jit(solution)/shard_map/all_gather | solution.py:32
  146.0 2.3 gather_fusion
  148.3 9.3 %all-to-all-start.2 = ((f32[64,1,4]{2,1,0:T(1,128)}), f32[64,1,4]{2,1,0:T(1,128)S(1)}, u32[]{:S(2)}, u32[]{:S(2)}) async-start(f32[64,1,4]{2,1,0:T(1,128)} %bitcast.3), calls=%async_computation.2 | async-start | bytes 65536 | tf_op jit(solution)/shard_map/all_to_all | solution.py:54
  157.6 2.0 fusion.11
  159.6 1.8 copy.16
  161.4 9.6 %all-to-all-done.2 = f32[64,1,4]{2,1,0:T(1,128)S(1)} async-done(((f32[64,1,4]{2,1,0:T(1,128)}), f32[64,1,4]{2,1,0:T(1,128)S(1)}, u32[]{:S(2)}, u32[]{:S(2)}) %all-to-all-start.2) | async-done | bytes 1056 | tf_op jit(solution)/shard_map/all_to_all | solution.py:54
  171.0 5.0 %all-to-all-start.1 = ((f32[64,4,256]{2,1,0:T(4,128)}), f32[64,4,256]{2,1,0:T(4,128)S(1)}, u32[]{:S(2)}, u32[]{:S(2)}) async-start(f32[64,4,256]{2,1,0:T(4,128)} %copy.16), calls=%async_computation.1 | async-start | bytes 524288 | tf_op jit(solution)/shard_map/all_to_all | solution.py:47
  176.5 0.7 reduce.7
  177.9 0.7 reduce.6
  178.9 14.6 %all-to-all-done.1 = f32[64,4,256]{2,1,0:T(4,128)S(1)} async-done(((f32[64,4,256]{2,1,0:T(4,128)}), f32[64,4,256]{2,1,0:T(4,128)S(1)}, u32[]{:S(2)}, u32[]{:S(2)}) %all-to-all-start.1) | async-done | bytes 262176 | tf_op jit(solution)/shard_map/all_to_all | solution.py:47
  193.5 0.8 fusion.6
  194.4 133.4 %all-gather.5.cloned.1.call-done = bf16[2048,256]{1,0:T(8,128)(2,1)} async-done(((bf16[32,256]{1,0:T(8,128)(2,1)}), bf16[2048,256]{1,0:T(8,128)(2,1)}) %all-gather.5.cloned.1.call-update) | async-done | bytes 1048592 | tf_op jit(solution)/shard_map/all_gather | solution.py:32
  327.9 2.3 gather_fusion.1
  330.3 2.1 fusion.3
  332.4 22.6 %psum.15 = f32[256]{0:T(256)S(1)} all-reduce(f32[256]{0:T(256)S(1)} %multiply_reduce_fusion), channel_id=1, replica_groups=mesh['pix'=64,'tm'=8] {'tm'}, use_global_device_ids=true, to_apply=%region_4.5 | all-reduce | flops 256 | bytes 2048 | tf_op jit(solution)/shard_map/psum | solution.py:82
  354.9 2.0 copy.18
  357.0 3.5 fusion.19
  360.5 68.1 %all-reduce.2.cloned.1.call-done = f32[256,128]{1,0:T(8,128)} async-done(((f32[256,128]{1,0:T(8,128)}), f32[256,128]{1,0:T(8,128)}) %all-reduce.2.cloned.1.call-update) | async-done | bytes 131088 | tf_op jit(solution)/shard_map/psum | solution.py:82
  428.6 1.7 fusion.23
  (26 shorter events, 4.8 us)
Async XLA Ops:
  7.2 138.8 %all-gather.3.cloned.1.call-start = ((), (), s32[]{:S(2)}) async-start(), calls=%async_computation.3 | async-start | bytes 1064960 | tf_op jit(solution)/shard_map/all_gather | solution.py:32
  9.3 139.0 %all-to-all-start = ((s32[64,1,4]{2,1,0:T(1,128)}), s32[64,1,4]{2,1,0:T(1,128)S(1)}, u32[]{:S(2)}, u32[]{:S(2)}) async-start(s32[64,1,4]{2,1,0:T(1,128)} %bitcast), calls=%async_computation | async-start | bytes 65536 | tf_op jit(solution)/shard_map/all_to_all | solution.py:26
  31.6 125.9 %copy-start = (bf16[2048,256]{1,0:T(8,128)(2,1)S(1)}, bf16[2048,256]{1,0:T(8,128)(2,1)}, u32[]{:S(2)}) copy-start(bf16[2048,256]{1,0:T(8,128)(2,1)} %param.6) | copy-start | bytes 3145732
  148.3 22.7 %all-to-all-start.2 = ((f32[64,1,4]{2,1,0:T(1,128)}), f32[64,1,4]{2,1,0:T(1,128)S(1)}, u32[]{:S(2)}, u32[]{:S(2)}) async-start(f32[64,1,4]{2,1,0:T(1,128)} %bitcast.3), calls=%async_computation.2 | async-start | bytes 65536 | tf_op jit(solution)/shard_map/all_to_all | solution.py:54
  157.6 35.9 %copy-start.1 = (bf16[32,256]{1,0:T(8,128)(2,1)S(1)}, bf16[32,256]{1,0:T(8,128)(2,1)}, u32[]{:S(2)}) copy-start(bf16[32,256]{1,0:T(8,128)(2,1)} %param.7) | copy-start | bytes 49156
  171.0 22.4 %all-to-all-start.1 = ((f32[64,4,256]{2,1,0:T(4,128)}), f32[64,4,256]{2,1,0:T(4,128)S(1)}, u32[]{:S(2)}, u32[]{:S(2)}) async-start(f32[64,4,256]{2,1,0:T(4,128)} %copy.16), calls=%async_computation.1 | async-start | bytes 524288 | tf_op jit(solution)/shard_map/all_to_all | solution.py:47
  176.0 151.9 %all-gather.5.cloned.1.call-start = ((), (), s32[]{:S(2)}) async-start(), calls=%async_computation.4 | async-start | bytes 1064960 | tf_op jit(solution)/shard_map/all_gather | solution.py:32
  194.4 234.2 %all-reduce.2.cloned.1.call-start = ((), (), s32[]{:S(2)}) async-start(), calls=%async_computation.5 | async-start | bytes 262144 | tf_op jit(solution)/shard_map/psum | solution.py:82
Sparse Core Ops, SparseCore 0:
  10.9 134.9 all-gather.2
  194.5 133.3 all-gather.4
  360.6 67.9 all-reduce.1
where the time goes:
time: 438 us; the launch traced here: 437 us
  waiting for transfers between devices  339 us (77%)
  starting transfers between devices  33.5 us (8%)
  blocking collectives  22.6 us (5%)
  between operations  13.9 us (3%)
  local copies, waits for them, and re-layouts  12.2 us (3%)
  matrix products  8.5 us (2%)
  other arithmetic  7.22 us (2%)
    all_gather x2, waiting for transfers between devices, slot_rows(): gathered = lax.all_gather(source_rows, 'pix', axis=0, tiled=True)  246 us
    psum x1, waiting for transfers between devices, local(): numer_all, power_all = lax.psum((numerator, trace_power), 'tm')  68.1 us
    psum x1, blocking collectives, local(): numer_all, power_all = lax.psum((numerator, trace_power), 'tm')  22.6 us
    all_to_all x1, starting transfers between devices, local(): lax.all_to_all(slot_neuron.reshape(pix_count, capacity), 'pix', split_axi...  19.1 us
    all_to_all x1, waiting for transfers between devices, local(): lax.all_to_all(projection.reshape(pix_count, capacity, projection.shape[1...  14.6 us
    all_to_all x1, waiting for transfers between devices, local(): lax.all_to_all(slot_power.reshape(pix_count, capacity), 'pix', split_axis...  9.56 us
    all_to_all x1, starting transfers between devices, local(): lax.all_to_all(slot_power.reshape(pix_count, capacity), 'pix', split_axis...  9.29 us
  transfers between devices with their start and end apart: 6, of which 5 were waited for; matrix products, arithmetic and copies ran while one was open for 3% of the time, Pallas kernels for 0%

commit v1 on v0

--- a/solution.py
+++ b/solution.py
@@ -8,9 +8,11 @@
 
 def local(movie, traces, footprints, slot_block, slot_neuron, bucket_fill):
     pix_count = lax.axis_size("pix")
+    tm_count = lax.axis_size("tm")
     slot_total = footprints.shape[0]
     capacity = slot_total // pix_count
     neur_local = traces.shape[0]
+    frames = traces.shape[1]
     block_count = movie.shape[0] // BLOCK
     slot_index = jnp.arange(slot_total, dtype=jnp.int32)
     bucket_of = slot_index // capacity
@@ -23,15 +25,17 @@
     dense_map = (block_pick.astype(jnp.bfloat16)[:, :, None] * masked[:, None, :]).reshape(
         slot_total, block_count * BLOCK
     )
-    asked_ids = lax.all_to_all(
+    asked = lax.all_to_all(
         slot_neuron.reshape(pix_count, capacity), "pix", split_axis=0, concat_axis=0, tiled=True
     )
-    asked_flat = asked_ids.reshape(slot_total)
+    asked_flat = asked.reshape(slot_total)
 
     def slot_rows(source_rows):
-        gathered = lax.all_gather(source_rows, "pix", axis=0, tiled=True)
-        global_row = bucket_of * neur_local + slot_neuron
-        return gathered[global_row]
+        picked = jnp.take(source_rows, asked_flat, axis=0, mode="clip")
+        got = lax.all_to_all(
+            picked.reshape(pix_count, capacity, frames), "pix", split_axis=0, concat_axis=0, tiled=True
+        )
+        return got.reshape(slot_total, frames)
 
     def residual_of(slot_traces):
         rebuilt = lax.dot_general(
@@ -43,27 +47,18 @@
     residual = residual_of(slot_traces)
     projection = jnp.dot(dense_map, residual, preferred_element_type=jnp.float32)
     slot_power = jnp.sum(masked.astype(jnp.float32) ** 2, axis=1)
-    got_proj, got_power = (
-        lax.all_to_all(
-            projection.reshape(pix_count, capacity, projection.shape[1]),
-            "pix",
-            split_axis=0,
-            concat_axis=0,
-            tiled=True,
-        ),
-        lax.all_to_all(
-            slot_power.reshape(pix_count, capacity), "pix", split_axis=0, concat_axis=0, tiled=True
-        ),
+    power_row = jnp.pad(
+        slot_power.reshape(pix_count, 1, capacity), ((0, 0), (0, 0), (0, frames - capacity))
     )
+    sent = jnp.concatenate([projection.reshape(pix_count, capacity, frames), power_row], axis=1)
+    got = lax.all_to_all(sent, "pix", split_axis=0, concat_axis=0, tiled=True)
+    got_proj = got[:, :capacity, :].reshape(slot_total, frames)
+    got_power = got[:, capacity, :capacity].reshape(slot_total)
     owner_pick = (jnp.arange(neur_local, dtype=jnp.int32)[:, None] == asked_flat[None, :]).astype(
         jnp.float32
     )
-    summed = jnp.dot(
-        owner_pick,
-        got_proj.reshape(slot_total, projection.shape[1]),
-        precision=lax.Precision.HIGHEST,
-    )
-    power = jnp.dot(owner_pick, got_power.reshape(slot_total), precision=lax.Precision.HIGHEST)
+    summed = jnp.dot(owner_pick, got_proj, precision=lax.Precision.HIGHEST)
+    power = jnp.dot(owner_pick, got_power, precision=lax.Precision.HIGHEST)
     updated = jnp.maximum(
         0.0, traces.astype(jnp.float32) + summed / jnp.maximum(power, 0.5)[:, None]
     ).astype(jnp.bfloat16)
@@ -79,7 +74,20 @@
         precision=lax.Precision.HIGHEST,
     )
     trace_power = jnp.sum(slot_updated.astype(jnp.float32) ** 2, axis=1)
-    numer_all, power_all = lax.psum((numerator, trace_power), "tm")
+    pl_rows = slot_total // BLOCK
+    stacked = jnp.concatenate([numerator, trace_power.reshape(pl_rows, BLOCK)], axis=0)
+    rows = stacked.shape[0]
+    chunk = -(-rows // tm_count)
+    stacked = jnp.pad(stacked, ((0, chunk * tm_count - rows), (0, 0)))
+    parts = lax.all_to_all(
+        stacked.reshape(tm_count, chunk, BLOCK), "tm", split_axis=0, concat_axis=0, tiled=True
+    )
+    mine = jnp.sum(parts, axis=0, keepdims=True)
+    whole = lax.all_to_all(
+        jnp.broadcast_to(mine, (tm_count, chunk, BLOCK)), "tm", split_axis=0, concat_axis=0, tiled=True
+    ).reshape(chunk * tm_count, BLOCK)
+    numer_all = whole[:slot_total]
+    power_all = whole[slot_total : slot_total + pl_rows].reshape(slot_total)
     grown = jnp.maximum(0.0, masked.astype(jnp.float32) + numer_all / (power_all + 1e-06)[:, None])
     return (updated, jnp.where(usable[:, None], grown, 0.0))
 

time: 438 us -> 150 us (0.34)
  waiting for transfers between devices: 339 us -> 24.9 us
  blocking collectives: 22.6 us -> 79.2 us
  between operations: 13.9 us -> 0.89 us
  starting transfers between devices: 33.5 us -> 23.7 us
    all_gather x2 -> x0, waiting for transfers between devices: 246 us -> none  [slot_rows(): gathered = lax.all_gather(source_rows, 'pix', axis=0, tiled=True)]
    all_to_all x0 -> x4, blocking collectives: none -> 79.2 us  [the longest x1 33.5 us: local(): got = lax.all_to_all(sent, 'pix', split_axis=0, concat_axis=0, tiled=True)]
    psum x1 -> x0, waiting for transfers between devices: 68.1 us -> none  [local(): numer_all, power_all = lax.psum((numerator, trace_power), 'tm')]
    psum x1 -> x0, blocking collectives: 22.6 us -> none  [local(): numer_all, power_all = lax.psum((numerator, trace_power), 'tm')]
    all_to_all x1, waiting for transfers between devices: 0.01 us -> 12.6 us  [local(): lax.all_to_all(slot_neuron.reshape(pix_count, capacity), 'pix', split_axi...]
    all_to_all x2 -> x1, waiting for transfers between devices: 24.1 us -> 12.2 us  [slot_rows(): lax.all_to_all(picked.reshape(pix_count, capacity, frames), 'pix', split_...]
    all_to_all x2 -> x1, starting transfers between devices: 14.3 us -> 4.62 us  [slot_rows(): lax.all_to_all(picked.reshape(pix_count, capacity, frames), 'pix', split_...]
  transfers between devices with their start and end apart: 6 -> 2, of which waited for: 5 -> 2; matrix products, arithmetic and copies ran while one was open for 3% -> 2% of each run, Pallas kernels for 0% -> 0%
where the time goes in v1:
time: 150 us; the launch traced here: 149 us
  blocking collectives  79.2 us (53%)
  waiting for transfers between devices  24.9 us (17%)
  starting transfers between devices  23.7 us (16%)
  local copies, waits for them, and re-layouts  8.98 us (6%)
  matrix products  6.51 us (4%)
  other arithmetic  4.99 us (3%)
    all_to_all x1, blocking collectives, local(): got = lax.all_to_all(sent, 'pix', split_axis=0, concat_axis=0, tiled=True)  33.5 us
    all_to_all x1, blocking collectives, slot_rows(): lax.all_to_all(picked.reshape(pix_count, capacity, frames), 'pix', split_...  23.7 us
    all_to_all x1, starting transfers between devices, local(): lax.all_to_all(slot_neuron.reshape(pix_count, capacity), 'pix', split_axi...  19.1 us
    all_to_all x1, blocking collectives, local(): lax.all_to_all(stacked.reshape(tm_count, chunk, BLOCK), 'tm', split_axis=...  13.2 us
    all_to_all x1, waiting for transfers between devices, local(): lax.all_to_all(slot_neuron.reshape(pix_count, capacity), 'pix', split_axi...  12.6 us
    all_to_all x1, waiting for transfers between devices, slot_rows(): lax.all_to_all(picked.reshape(pix_count, capacity, frames), 'pix', split_...  12.2 us
    all_to_all x1, blocking collectives, local(): lax.all_to_all(jnp.broadcast_to(mine, (tm_count, chunk, BLOCK)), 'tm', sp...  8.85 us
    all_to_all x1, starting transfers between devices, slot_rows(): lax.all_to_all(picked.reshape(pix_count, capacity, frames), 'pix', split_...  4.62 us
  transfers between devices with their start and end apart: 2, of which 2 were waited for; matrix products, arithmetic and copies ran while one was open for 2% of the time, Pallas kernels for 0%

profile of v1, /device:TPU:1, one launch (start us, length us, event | category | flops | bytes accessed | tf_op | source)
XLA Modules:
  0.0 149.1 jit_solution(2737108121999394802)
XLA Ops:
  0.6 1.4 all_to_all.21
  2.0 19.1 %all-to-all-start = ((s32[64,1,4]{2,1,0:T(1,128)}), s32[64,1,4]{2,1,0:T(1,128)S(1)}, u32[]{:S(2)}, u32[]{:S(2)}) async-start(s32[64,1,4]{2,1,0:T(1,128)} %bitcast), calls=%async_computation | async-start | bytes 65536 | tf_op jit(solution)/shard_map/all_to_all | solution.py:28
  21.1 0.7 select_reduce_fusion
  21.9 12.6 %all-to-all-done = s32[64,1,4]{2,1,0:T(1,128)S(1)} async-done(((s32[64,1,4]{2,1,0:T(1,128)}), s32[64,1,4]{2,1,0:T(1,128)S(1)}, u32[]{:S(2)}, u32[]{:S(2)}) %all-to-all-start) | async-done | bytes 1056 | tf_op jit(solution)/shard_map/all_to_all | solution.py:28
  34.5 0.5 broadcast.119
  35.1 0.7 reduce.8
  35.9 1.7 %gather_fusion = bf16[256,256]{1,0:T(8,128)(2,1)S(1)} fusion(bf16[32,256]{1,0:T(8,128)(2,1)} %param.7, s32[1024]{0:T(1024)S(1)} %pad_clamp_fusion), kind=kCustom, calls=%fused_computation | custom fusion | bytes 263168 | tf_op jit(solution)/shard_map/jit(_take)/gather | solution.py:34
  37.6 0.7 reshape.130
  38.3 4.6 %all-to-all-start.1 = ((bf16[64,4,256]{2,1,0:T(4,128)(2,1)}), bf16[64,4,256]{2,1,0:T(4,128)(2,1)S(1)}, u32[]{:S(2)}, u32[]{:S(2)}) async-start(bf16[64,4,256]{2,1,0:T(4,128)(2,1)} %reshape.130), calls=%async_computation.1 | async-start | bytes 262144 | tf_op jit(solution)/shard_map/all_to_all | solution.py:35
  42.9 1.0 fusion.18
  44.1 0.8 fusion.21
  44.8 0.7 broadcast_multiply_fusion
  45.8 12.2 %all-to-all-done.1 = bf16[64,4,256]{2,1,0:T(4,128)(2,1)S(1)} async-done(((bf16[64,4,256]{2,1,0:T(4,128)(2,1)}), bf16[64,4,256]{2,1,0:T(4,128)(2,1)S(1)}, u32[]{:S(2)}, u32[]{:S(2)}) %all-to-all-start.1) | async-done | bytes 131104 | tf_op jit(solution)/shard_map/all_to_all | solution.py:35
  58.1 2.5 %fusion.9 = f32[64,4,256]{2,0,1:T(8,128)S(1)} fusion(bf16[64,4,2048]{2,1,0:T(4,128)(2,1)S(1)} %mul.44, bf16[256,256]{1,0:T(8,128)(2,1)S(1)} %reshape.131, bf16[2048,256]{1,0:T(8,128)(2,1)} %param.6, bf16[32,8,16,128]{3,2,1,0:T(8,128)(2,1)S(1)} %bitcast.32), kind=kOutput, calls=%fused_computation.15 | convolution fusion | flops 538443776 | bytes 3538944 | tf_op jit(solution)/shard_map/dot_general | solution.py:48
  60.9 33.5 %all_to_all.34 = f32[64,5,256]{2,1,0:T(8,128)S(1)} all-to-all(f32[64,5,256]{2,1,0:T(8,128)S(1)} %copy.15), channel_id=1, replica_groups=mesh['pix'=64,'tm'=8] {'pix'}, dimensions={0} | all-to-all | bytes 655360 | tf_op jit(solution)/shard_map/all_to_all | solution.py:54
  95.2 1.2 gather_fusion.1
  96.4 23.7 %all_to_all.35 = bf16[64,4,256]{2,1,0:T(4,128)(2,1)S(1)} all-to-all(bf16[64,4,256]{2,1,0:T(4,128)(2,1)S(1)} %reshape.134), channel_id=1, replica_groups=mesh['pix'=64,'tm'=8] {'pix'}, dimensions={0} | all-to-all | bytes 262144 | tf_op jit(solution)/shard_map/all_to_all | solution.py:35
  120.3 0.6 fusion.1
  121.0 1.8 %fusion.30 = f32[16,128,256]{2,1,0:T(8,128)} fusion(bf16[16,128,256]{2,1,0:T(8,128)(2,1)S(1)} %bitcast.34, bf16[256,256,1]{1,0,2:T(8,128)(2,1)S(1)} %reshape.160), kind=kOutput, calls=%fused_computation.54 | convolution fusion | flops 268435456 | bytes 3276800 | tf_op jit(solution)/shard_map/dot_general | solution.py:67
  122.8 2.2 %copy.16 = f32[16,128,256]{1,0,2:T(8,128)S(1)} copy(f32[16,128,256]{2,1,0:T(8,128)} %fusion.30) | data formatting | bytes 4194304 | tf_op jit(solution)/shard_map/dot_general | solution.py:67
  125.0 1.2 fusion.16
  126.2 13.2 %all_to_all.36 = f32[8,33,128]{2,1,0:T(8,128)S(1)} all-to-all(f32[8,33,128]{2,1,0:T(8,128)S(1)} %reshape.137), channel_id=1, replica_groups=mesh['pix'=64,'tm'=8] {'tm'}, dimensions={0} | all-to-all | bytes 270336 | tf_op jit(solution)/shard_map/all_to_all | solution.py:82
  139.5 8.8 %all_to_all.37 = f32[8,33,128]{2,1,0:T(8,128)S(1)} all-to-all(f32[8,33,128]{2,1,0:T(8,128)S(1)} %broadcast_in_dim.51), channel_id=1, replica_groups=mesh['pix'=64,'tm'=8] {'tm'}, dimensions={0} | all-to-all | bytes 270336 | tf_op jit(solution)/shard_map/all_to_all | solution.py:86
  148.3 0.8 fusion.20
  (32 shorter events, 1.9 us)
Async XLA Ops:
  2.0 32.5 %all-to-all-start = ((s32[64,1,4]{2,1,0:T(1,128)}), s32[64,1,4]{2,1,0:T(1,128)S(1)}, u32[]{:S(2)}, u32[]{:S(2)}) async-start(s32[64,1,4]{2,1,0:T(1,128)} %bitcast), calls=%async_computation | async-start | bytes 65536 | tf_op jit(solution)/shard_map/all_to_all | solution.py:28
  38.3 19.8 %all-to-all-start.1 = ((bf16[64,4,256]{2,1,0:T(4,128)(2,1)}), bf16[64,4,256]{2,1,0:T(4,128)(2,1)S(1)}, u32[]{:S(2)}, u32[]{:S(2)}) async-start(bf16[64,4,256]{2,1,0:T(4,128)(2,1)} %reshape.130), calls=%async_computation.1 | async-start | bytes 262144 | tf_op jit(solution)/shard_map/all_to_all | solution.py:35
  60.7 34.2 %copy-start = (bf16[32,256]{1,0:T(8,128)(2,1)S(1)}, bf16[32,256]{1,0:T(8,128)(2,1)}, u32[]{:S(2)}) copy-start(bf16[32,256]{1,0:T(8,128)(2,1)} %param.7) | copy-start | bytes 49156
  60.9 59.4 %copy-start.2 = (bf16[2048,256]{1,0:T(8,128)(2,1)S(1)}, bf16[2048,256]{1,0:T(8,128)(2,1)}, u32[]{:S(2)}) copy-start(bf16[2048,256]{1,0:T(8,128)(2,1)} %param.6) | copy-start | bytes 3145732
  95.2 25.8 %copy-start.1 = (bf16[32,256]{1,0:T(8,128)(2,1)}, bf16[32,256]{1,0:T(8,128)(2,1)S(1)}, u32[]{:S(2)}) copy-start(bf16[32,256]{1,0:T(8,128)(2,1)S(1)} %fusion.5) | copy-start | bytes 49156

commit v2 on v1

--- a/solution.py
+++ b/solution.py
@@ -25,10 +25,22 @@
     dense_map = (block_pick.astype(jnp.bfloat16)[:, :, None] * masked[:, None, :]).reshape(
         slot_total, block_count * BLOCK
     )
-    asked = lax.all_to_all(
-        slot_neuron.reshape(pix_count, capacity), "pix", split_axis=0, concat_axis=0, tiled=True
+    slot_power = jnp.sum(masked.astype(jnp.float32) ** 2, axis=1)
+    asked_and_power = lax.all_to_all(
+        jnp.concatenate(
+            [
+                slot_neuron.astype(jnp.float32).reshape(pix_count, capacity),
+                slot_power.reshape(pix_count, capacity),
+            ],
+            axis=1,
+        ),
+        "pix",
+        split_axis=0,
+        concat_axis=0,
+        tiled=True,
     )
-    asked_flat = asked.reshape(slot_total)
+    asked_flat = asked_and_power[:, :capacity].astype(jnp.int32).reshape(slot_total)
+    got_power = asked_and_power[:, capacity:].reshape(slot_total)
 
     def slot_rows(source_rows):
         picked = jnp.take(source_rows, asked_flat, axis=0, mode="clip")
@@ -46,14 +58,9 @@
     slot_traces = slot_rows(traces)
     residual = residual_of(slot_traces)
     projection = jnp.dot(dense_map, residual, preferred_element_type=jnp.float32)
-    slot_power = jnp.sum(masked.astype(jnp.float32) ** 2, axis=1)
-    power_row = jnp.pad(
-        slot_power.reshape(pix_count, 1, capacity), ((0, 0), (0, 0), (0, frames - capacity))
-    )
-    sent = jnp.concatenate([projection.reshape(pix_count, capacity, frames), power_row], axis=1)
-    got = lax.all_to_all(sent, "pix", split_axis=0, concat_axis=0, tiled=True)
-    got_proj = got[:, :capacity, :].reshape(slot_total, frames)
-    got_power = got[:, capacity, :capacity].reshape(slot_total)
+    got_proj = lax.all_to_all(
+        projection.reshape(pix_count, capacity, frames), "pix", split_axis=0, concat_axis=0, tiled=True
+    ).reshape(slot_total, frames)
     owner_pick = (jnp.arange(neur_local, dtype=jnp.int32)[:, None] == asked_flat[None, :]).astype(
         jnp.float32
     )

time: 150 us -> 139 us (0.927)
  starting transfers between devices: 23.7 us -> 9.79 us
  waiting for transfers between devices: 24.9 us -> 31.7 us
  blocking collectives: 79.2 us -> 77.5 us
    all_to_all x1, starting transfers between devices: 19.1 us -> 5.17 us  [local(): lax.all_to_all(projection.reshape(pix_count, capacity, frames), 'pix', sp...]
    all_to_all x1, waiting for transfers between devices: 12.6 us -> 17.7 us  [local(): lax.all_to_all(projection.reshape(pix_count, capacity, frames), 'pix', sp...]
    all_to_all x2 -> x0, local copies, waits for them, and re-layouts: 1.91 us -> none  [local(): lax.all_to_all(slot_neuron.reshape(pix_count, capacity), 'pix', split_axi...]
    all_to_all x1, waiting for transfers between devices: 12.2 us -> 14 us  [slot_rows(): lax.all_to_all(picked.reshape(pix_count, capacity, frames), 'pix', split_...]
  transfers between devices with their start and end apart: 2 -> 2, of which waited for: 2 -> 2; matrix products, arithmetic and copies ran while one was open for 2% -> 1% of each run, Pallas kernels for 0% -> 0%
where the time goes in v2:
time: 139 us; the launch traced here: 138 us
  blocking collectives  77.5 us (56%)
  waiting for transfers between devices  31.7 us (23%)
  starting transfers between devices  9.79 us (7%)
  local copies, waits for them, and re-layouts  7.74 us (6%)
  matrix products  6.49 us (5%)
  other arithmetic  4.4 us (3%)
    all_to_all x1, blocking collectives, local(): lax.all_to_all(jnp.concatenate([slot_neuron.astype(jnp.float32).reshape(p...  32.4 us
    all_to_all x1, blocking collectives, slot_rows(): lax.all_to_all(picked.reshape(pix_count, capacity, frames), 'pix', split_...  22.3 us
    all_to_all x1, waiting for transfers between devices, local(): lax.all_to_all(projection.reshape(pix_count, capacity, frames), 'pix', sp...  17.7 us
    all_to_all x1, waiting for transfers between devices, slot_rows(): lax.all_to_all(picked.reshape(pix_count, capacity, frames), 'pix', split_...  14 us
    all_to_all x1, blocking collectives, local(): lax.all_to_all(stacked.reshape(tm_count, chunk, BLOCK), 'tm', split_axis=...  14 us
    all_to_all x1, blocking collectives, local(): lax.all_to_all(jnp.broadcast_to(mine, (tm_count, chunk, BLOCK)), 'tm', sp...  8.85 us
    all_to_all x1, starting transfers between devices, local(): lax.all_to_all(projection.reshape(pix_count, capacity, frames), 'pix', sp...  5.17 us
    all_to_all x1, starting transfers between devices, slot_rows(): lax.all_to_all(picked.reshape(pix_count, capacity, frames), 'pix', split_...  4.62 us
  transfers between devices with their start and end apart: 2, of which 2 were waited for; matrix products, arithmetic and copies ran while one was open for 1% of the time, Pallas kernels for 0%

profile of v2, /device:TPU:1, one launch (start us, length us, event | category | flops | bytes accessed | tf_op | source)
XLA Modules:
  0.0 138.5 jit_solution(2538099763960698402)
XLA Ops:
  0.6 0.7 convert_element_type.50
  1.3 0.7 select_reduce_fusion
  2.2 1.0 fusion.18
  3.4 32.4 %all_to_all.37 = f32[64,1,8]{2,1,0:T(1,128)S(1)} all-to-all(f32[64,1,8]{2,1,0:T(1,128)S(1)} %bitcast.40), channel_id=1, replica_groups=mesh['pix'=64,'tm'=8] {'pix'}, dimensions={0} | all-to-all | bytes 4096 | tf_op jit(solution)/shard_map/all_to_all | solution.py:29
  36.0 1.7 %gather_fusion = bf16[256,256]{1,0:T(8,128)(2,1)S(1)} fusion(bf16[32,256]{1,0:T(8,128)(2,1)} %param.7, s32[1024]{0:T(1024)S(1)} %pad_clamp_fusion), kind=kCustom, calls=%fused_computation | custom fusion | bytes 263168 | tf_op jit(solution)/shard_map/jit(_take)/gather | solution.py:46
  37.7 0.7 reshape.134
  38.4 4.6 %all-to-all-start.1 = ((bf16[64,4,256]{2,1,0:T(4,128)(2,1)}), bf16[64,4,256]{2,1,0:T(4,128)(2,1)S(1)}, u32[]{:S(2)}, u32[]{:S(2)}) async-start(bf16[64,4,256]{2,1,0:T(4,128)(2,1)} %reshape.134), calls=%async_computation.1 | async-start | bytes 262144 | tf_op jit(solution)/shard_map/all_to_all | solution.py:47
  43.1 0.7 broadcast_multiply_fusion
  43.8 0.3 mul.44
  44.1 14.0 %all-to-all-done.1 = bf16[64,4,256]{2,1,0:T(4,128)(2,1)S(1)} async-done(((bf16[64,4,256]{2,1,0:T(4,128)(2,1)}), bf16[64,4,256]{2,1,0:T(4,128)(2,1)S(1)}, u32[]{:S(2)}, u32[]{:S(2)}) %all-to-all-start.1) | async-done | bytes 131104 | tf_op jit(solution)/shard_map/all_to_all | solution.py:47
  58.2 2.5 %fusion.9 = f32[64,4,256]{2,0,1:T(8,128)S(1)} fusion(bf16[64,4,2048]{2,1,0:T(4,128)(2,1)S(1)} %mul.44, bf16[256,256]{1,0:T(8,128)(2,1)S(1)} %reshape.135, bf16[2048,256]{1,0:T(8,128)(2,1)} %param.6, bf16[32,8,16,128]{3,2,1,0:T(8,128)(2,1)S(1)} %bitcast.35), kind=kOutput, calls=%fused_computation.15 | convolution fusion | flops 538443776 | bytes 3538944 | tf_op jit(solution)/shard_map/dot_general | solution.py:60
  60.7 0.9 copy.17
  61.6 5.2 %all-to-all-start.2 = ((f32[64,4,256]{2,1,0:T(4,128)}), f32[64,4,256]{2,1,0:T(4,128)S(1)}, u32[]{:S(2)}, u32[]{:S(2)}) async-start(f32[64,4,256]{2,1,0:T(4,128)} %copy.17), calls=%async_computation.2 | async-start | bytes 524288 | tf_op jit(solution)/shard_map/all_to_all | solution.py:61
  67.0 17.7 %all-to-all-done.2 = f32[64,4,256]{2,1,0:T(4,128)S(1)} async-done(((f32[64,4,256]{2,1,0:T(4,128)}), f32[64,4,256]{2,1,0:T(4,128)S(1)}, u32[]{:S(2)}, u32[]{:S(2)}) %all-to-all-start.2) | async-done | bytes 262176 | tf_op jit(solution)/shard_map/all_to_all | solution.py:61
  84.8 0.2 fusion.5
  85.0 1.2 gather_fusion.1
  86.2 22.3 %all_to_all.38 = bf16[64,4,256]{2,1,0:T(4,128)(2,1)S(1)} all-to-all(bf16[64,4,256]{2,1,0:T(4,128)(2,1)S(1)} %reshape.138), channel_id=1, replica_groups=mesh['pix'=64,'tm'=8] {'pix'}, dimensions={0} | all-to-all | bytes 262144 | tf_op jit(solution)/shard_map/all_to_all | solution.py:47
  108.9 0.6 fusion.1
  109.5 1.8 %fusion.31 = f32[16,128,256]{2,1,0:T(8,128)} fusion(bf16[16,128,256]{2,1,0:T(8,128)(2,1)S(1)} %bitcast.37, bf16[256,256,1]{1,0,2:T(8,128)(2,1)S(1)} %reshape.164), kind=kOutput, calls=%fused_computation.54 | convolution fusion | flops 268435456 | bytes 3276800 | tf_op jit(solution)/shard_map/dot_general | solution.py:74
  111.3 2.2 %copy.18 = f32[16,128,256]{1,0,2:T(8,128)S(1)} copy(f32[16,128,256]{2,1,0:T(8,128)} %fusion.31) | data formatting | bytes 4194304 | tf_op jit(solution)/shard_map/dot_general | solution.py:74
  113.6 1.2 fusion.16
  114.8 14.0 %all_to_all.39 = f32[8,33,128]{2,1,0:T(8,128)S(1)} all-to-all(f32[8,33,128]{2,1,0:T(8,128)S(1)} %reshape.141), channel_id=1, replica_groups=mesh['pix'=64,'tm'=8] {'tm'}, dimensions={0} | all-to-all | bytes 270336 | tf_op jit(solution)/shard_map/all_to_all | solution.py:89
  128.8 8.8 %all_to_all.40 = f32[8,33,128]{2,1,0:T(8,128)S(1)} all-to-all(f32[8,33,128]{2,1,0:T(8,128)S(1)} %broadcast_in_dim.51), channel_id=1, replica_groups=mesh['pix'=64,'tm'=8] {'tm'}, dimensions={0} | all-to-all | bytes 270336 | tf_op jit(solution)/shard_map/all_to_all | solution.py:93
  137.7 0.8 fusion.20
  (32 shorter events, 1.4 us)
Async XLA Ops:
  0.6 42.4 %copy-start.2 = (s32[256]{0:T(256)S(1)}, s32[256]{0:T(256)}, u32[]{:S(2)}) copy-start(s32[256]{0:T(256)} %param.9) | copy-start | bytes 3076
  38.4 19.8 %all-to-all-start.1 = ((bf16[64,4,256]{2,1,0:T(4,128)(2,1)}), bf16[64,4,256]{2,1,0:T(4,128)(2,1)S(1)}, u32[]{:S(2)}, u32[]{:S(2)}) async-start(bf16[64,4,256]{2,1,0:T(4,128)(2,1)} %reshape.134), calls=%async_computation.1 | async-start | bytes 262144 | tf_op jit(solution)/shard_map/all_to_all | solution.py:47
  58.2 26.6 %copy-start = (bf16[32,256]{1,0:T(8,128)(2,1)S(1)}, bf16[32,256]{1,0:T(8,128)(2,1)}, u32[]{:S(2)}) copy-start(bf16[32,256]{1,0:T(8,128)(2,1)} %param.7) | copy-start | bytes 49156
  61.6 47.3 %copy-start.3 = (bf16[2048,256]{1,0:T(8,128)(2,1)S(1)}, bf16[2048,256]{1,0:T(8,128)(2,1)}, u32[]{:S(2)}) copy-start(bf16[2048,256]{1,0:T(8,128)(2,1)} %param.6) | copy-start | bytes 3145732
  61.6 23.1 %all-to-all-start.2 = ((f32[64,4,256]{2,1,0:T(4,128)}), f32[64,4,256]{2,1,0:T(4,128)S(1)}, u32[]{:S(2)}, u32[]{:S(2)}) async-start(f32[64,4,256]{2,1,0:T(4,128)} %copy.17), calls=%async_computation.2 | async-start | bytes 524288 | tf_op jit(solution)/shard_map/all_to_all | solution.py:61
  85.0 24.4 %copy-start.1 = (bf16[32,256]{1,0:T(8,128)(2,1)}, bf16[32,256]{1,0:T(8,128)(2,1)S(1)}, u32[]{:S(2)}) copy-start(bf16[32,256]{1,0:T(8,128)(2,1)S(1)} %fusion.5) | copy-start | bytes 49156

commit v3 on v2

--- a/solution.py
+++ b/solution.py
@@ -17,8 +17,7 @@
     slot_index = jnp.arange(slot_total, dtype=jnp.int32)
     bucket_of = slot_index // capacity
     position = slot_index % capacity
-    owner_match = bucket_of[:, None] == jnp.arange(pix_count, dtype=jnp.int32)[None, :]
-    fill_slot = jnp.sum(jnp.where(owner_match, bucket_fill[0][None, :], 0), axis=1)
+    fill_slot = jnp.repeat(bucket_fill[0], capacity, total_repeat_length=slot_total)
     usable = position < fill_slot
     masked = footprints * usable[:, None].astype(jnp.bfloat16)
     block_pick = slot_block[:, None] == jnp.arange(block_count, dtype=jnp.int32)[None, :]
@@ -39,14 +38,18 @@
         concat_axis=0,
         tiled=True,
     )
-    asked_flat = asked_and_power[:, :capacity].astype(jnp.int32).reshape(slot_total)
+    asked = asked_and_power[:, :capacity].astype(jnp.int32)
+    asked_flat = asked.reshape(slot_total)
+    row_pick = (asked[:, :, None] == jnp.arange(neur_local, dtype=jnp.int32)[None, None, :]).astype(
+        jnp.bfloat16
+    )
     got_power = asked_and_power[:, capacity:].reshape(slot_total)
 
     def slot_rows(source_rows):
-        picked = jnp.take(source_rows, asked_flat, axis=0, mode="clip")
-        got = lax.all_to_all(
-            picked.reshape(pix_count, capacity, frames), "pix", split_axis=0, concat_axis=0, tiled=True
-        )
+        picked = jnp.einsum(
+            "okn,nf->okf", row_pick, source_rows, preferred_element_type=jnp.float32
+        ).astype(source_rows.dtype)
+        got = lax.all_to_all(picked, "pix", split_axis=0, concat_axis=0, tiled=True)
         return got.reshape(slot_total, frames)
 
     def residual_of(slot_traces):
@@ -57,9 +60,14 @@
 
     slot_traces = slot_rows(traces)
     residual = residual_of(slot_traces)
-    projection = jnp.dot(dense_map, residual, preferred_element_type=jnp.float32)
+    projection = jnp.einsum(
+        "okp,pf->okf",
+        dense_map.reshape(pix_count, capacity, block_count * BLOCK),
+        residual,
+        preferred_element_type=jnp.float32,
+    )
     got_proj = lax.all_to_all(
-        projection.reshape(pix_count, capacity, frames), "pix", split_axis=0, concat_axis=0, tiled=True
+        projection, "pix", split_axis=0, concat_axis=0, tiled=True
     ).reshape(slot_total, frames)
     owner_pick = (jnp.arange(neur_local, dtype=jnp.int32)[:, None] == asked_flat[None, :]).astype(
         jnp.float32
@@ -72,14 +80,9 @@
     slot_updated = slot_rows(updated)
     residual_two = residual_of(slot_updated)
     products = lax.dot_general(
-        residual_two, slot_updated, (((1,), (1,)), ((), ())), preferred_element_type=jnp.float32
-    )
-    numerator = jnp.einsum(
-        "bps,sb->sp",
-        products.reshape(block_count, BLOCK, slot_total),
-        block_pick.astype(jnp.float32),
-        precision=lax.Precision.HIGHEST,
-    )
+        slot_updated, residual_two, (((1,), (1,)), ((), ())), preferred_element_type=jnp.float32
+    ).reshape(slot_total, block_count, BLOCK)
+    numerator = jnp.sum(jnp.where(block_pick[:, :, None], products, 0.0), axis=1)
     trace_power = jnp.sum(slot_updated.astype(jnp.float32) ** 2, axis=1)
     pl_rows = slot_total // BLOCK
     stacked = jnp.concatenate([numerator, trace_power.reshape(pl_rows, BLOCK)], axis=0)

time: 139 us -> 136 us (0.978)
  local copies, waits for them, and re-layouts: 7.74 us -> 4.98 us
    dot_general x2 -> x1, local copies, waits for them, and re-layouts: 3.11 us -> 0.86 us  [local(): jnp.einsum('okp,pf->okf', dense_map.reshape(pix_count, capacity, block_co...]
    gather x2 -> x1, local copies, waits for them, and re-layouts: 2.84 us -> 1.87 us  [local(): jnp.repeat(bucket_fill[0], capacity, total_repeat_length=slot_total)]
    dot_general x3 -> x4, matrix products: 5.57 us -> 5.22 us  [the longest x1 2.52 us: local(): jnp.einsum('okp,pf->okf', dense_map.reshape(pix_count, capacity, block_co...]
where the time goes in v3:
time: 136 us; the launch traced here: 135 us
  blocking collectives  77.7 us (57%)
  waiting for transfers between devices  31.5 us (23%)
  starting transfers between devices  9.66 us (7%)
  matrix products  7.09 us (5%)
  local copies, waits for them, and re-layouts  4.98 us (4%)
  other arithmetic  3.54 us (3%)
    all_to_all x1, blocking collectives, local(): lax.all_to_all(jnp.concatenate([slot_neuron.astype(jnp.float32).reshape(p...  32.4 us
    all_to_all x1, blocking collectives, slot_rows(): got = lax.all_to_all(picked, 'pix', split_axis=0, concat_axis=0, tiled=True)  22.3 us
    all_to_all x1, waiting for transfers between devices, local(): lax.all_to_all(projection, 'pix', split_axis=0, concat_axis=0, tiled=True)  17.5 us
    all_to_all x1, blocking collectives, local(): lax.all_to_all(stacked.reshape(tm_count, chunk, BLOCK), 'tm', split_axis=...  14.2 us
    all_to_all x1, waiting for transfers between devices, slot_rows(): got = lax.all_to_all(picked, 'pix', split_axis=0, concat_axis=0, tiled=True)  14 us
    all_to_all x1, blocking collectives, local(): lax.all_to_all(jnp.broadcast_to(mine, (tm_count, chunk, BLOCK)), 'tm', sp...  8.85 us
    all_to_all x1, starting transfers between devices, local(): lax.all_to_all(projection, 'pix', split_axis=0, concat_axis=0, tiled=True)  5.04 us
    all_to_all x1, starting transfers between devices, slot_rows(): got = lax.all_to_all(picked, 'pix', split_axis=0, concat_axis=0, tiled=True)  4.62 us
  transfers between devices with their start and end apart: 2, of which 2 were waited for; matrix products, arithmetic and copies ran while one was open for 1% of the time, Pallas kernels for 0%

profile of v3, /device:TPU:1, one launch (start us, length us, event | category | flops | bytes accessed | tf_op | source)
XLA Modules:
  0.0 135.4 jit_solution(4799560528204182509)
XLA Ops:
  0.7 0.7 convert_element_type.56
  1.4 0.7 add_add_fusion.1
  2.2 1.9 %gather_fusion = s32[256]{0:T(256)S(1)} fusion(s32[64]{0:T(128)S(1)} %bitcast.45, s32[1024]{0:T(1024)S(1)} %pad_clamp_fusion), kind=kCustom, calls=%fused_computation | custom fusion | bytes 3072 | tf_op jit(solution)/shard_map/jit(_take)/gather | solution.py:20
  4.3 0.2 fusion.16
  4.6 32.4 %all_to_all.37 = f32[64,1,8]{2,1,0:T(1,128)S(1)} all-to-all(f32[64,1,8]{2,1,0:T(1,128)S(1)} %bitcast.49), channel_id=1, replica_groups=mesh['pix'=64,'tm'=8] {'pix'}, dimensions={0} | all-to-all | bytes 4096 | tf_op jit(solution)/shard_map/all_to_all | solution.py:28
  37.2 0.2 convolution_convert_fusion.1
  37.4 0.8 copy.38
  38.2 4.6 %all-to-all-start.1 = ((bf16[64,4,256]{2,1,0:T(4,128)(2,1)}), bf16[64,4,256]{2,1,0:T(4,128)(2,1)S(1)}, u32[]{:S(2)}, u32[]{:S(2)}) async-start(bf16[64,4,256]{2,1,0:T(4,128)(2,1)} %copy.38), calls=%async_computation.1 | async-start | bytes 262144 | tf_op jit(solution)/shard_map/all_to_all | solution.py:52
  42.9 0.7 broadcast_multiply_fusion
  43.7 0.3 mul.44
  44.0 14.0 %all-to-all-done.1 = bf16[64,4,256]{2,1,0:T(4,128)(2,1)S(1)} async-done(((bf16[64,4,256]{2,1,0:T(4,128)(2,1)}), bf16[64,4,256]{2,1,0:T(4,128)(2,1)S(1)}, u32[]{:S(2)}, u32[]{:S(2)}) %all-to-all-start.1) | async-done | bytes 131104 | tf_op jit(solution)/shard_map/all_to_all | solution.py:52
  58.0 2.5 %fusion.9 = f32[64,4,256]{2,0,1:T(8,128)S(1)} fusion(bf16[64,4,2048]{2,1,0:T(4,128)(2,1)S(1)} %mul.44, bf16[256,256]{1,0:T(8,128)(2,1)S(1)} %reshape.221, bf16[2048,256]{1,0:T(8,128)(2,1)} %param.8, bf16[32,8,16,128]{3,2,1,0:T(8,128)(2,1)S(1)} %bitcast.46), kind=kOutput, calls=%fused_computation.17 | convolution fusion | flops 538443776 | bytes 3538944 | tf_op jit(solution)/shard_map/okp,pf->okf/dot_general | solution.py:63
  60.5 0.9 copy.40
  61.4 5.0 %all-to-all-start.2 = ((f32[64,4,256]{2,1,0:T(4,128)}), f32[64,4,256]{2,1,0:T(4,128)S(1)}, u32[]{:S(2)}, u32[]{:S(2)}) async-start(f32[64,4,256]{2,1,0:T(4,128)} %copy.40), calls=%async_computation.2 | async-start | bytes 524288 | tf_op jit(solution)/shard_map/all_to_all | solution.py:69
  66.7 0.1 fusion.6
  66.8 17.5 %all-to-all-done.2 = f32[64,4,256]{2,1,0:T(4,128)S(1)} async-done(((f32[64,4,256]{2,1,0:T(4,128)}), f32[64,4,256]{2,1,0:T(4,128)S(1)}, u32[]{:S(2)}, u32[]{:S(2)}) %all-to-all-start.2) | async-done | bytes 262176 | tf_op jit(solution)/shard_map/all_to_all | solution.py:69
  84.4 0.2 fusion.5
  84.7 0.2 convolution_convert_fusion
  85.0 22.3 %all_to_all.38 = bf16[64,4,256]{2,1,0:T(4,128)(2,1)S(1)} all-to-all(bf16[64,4,256]{2,1,0:T(4,128)(2,1)S(1)} %copy.41), channel_id=1, replica_groups=mesh['pix'=64,'tm'=8] {'pix'}, dimensions={0} | all-to-all | bytes 262144 | tf_op jit(solution)/shard_map/all_to_all | solution.py:52
  107.7 1.5 %fusion.1 = bf16[2048,256]{1,0:T(8,128)(2,1)} fusion(bf16[256,256]{1,0:T(8,128)(2,1)S(1)} %reshape.224, bf16[2048,256]{1,0:T(8,128)(2,1)S(1)} %copy-done.6, bf16[32,8,16,128]{3,2,1,0:T(8,128)(2,1)S(1)} %bitcast.47), kind=kOutput, calls=%fused_computation.4 | convolution fusion | flops 270008320 | bytes 3276800 | tf_op jit(solution)/shard_map/dot_general | solution.py:56
  109.2 2.2 %select_reduce_fusion = f32[256,128]{1,0:T(8,128)S(1)} fusion(bf16[256,256,1]{1,0,2:T(8,128)(2,1)S(1)} %reshape.241, bf16[16,128,256]{2,1,0:T(8,128)(2,1)} %bitcast.53, pred[256,16]{0,1:T(8,128)(4,1)S(1)} %get-tuple-element.22), kind=kOutput, calls=%fused_computation.6 | convolution fusion | flops 269451264 | bytes 1314816 | tf_op jit(solution)/shard_map/dot_general | solution.py:82
  111.5 14.2 %all_to_all.39 = f32[8,33,128]{2,1,0:T(8,128)S(1)} all-to-all(f32[8,33,128]{2,1,0:T(8,128)S(1)} %reshape.226), channel_id=1, replica_groups=mesh['pix'=64,'tm'=8] {'tm'}, dimensions={0} | all-to-all | bytes 270336 | tf_op jit(solution)/shard_map/all_to_all | solution.py:92
  125.8 8.8 %all_to_all.40 = f32[8,33,128]{2,1,0:T(8,128)S(1)} all-to-all(f32[8,33,128]{2,1,0:T(8,128)S(1)} %broadcast_in_dim.30), channel_id=1, replica_groups=mesh['pix'=64,'tm'=8] {'tm'}, dimensions={0} | all-to-all | bytes 270336 | tf_op jit(solution)/shard_map/all_to_all | solution.py:96
  134.6 0.8 fusion.18
  (41 shorter events, 1.6 us)
Async XLA Ops:
  0.6 1.5 %copy-start = (s32[1,64]{1,0:T(1,128)S(1)}, s32[1,64]{1,0:T(1,128)}, u32[]{:S(2)}) copy-start(s32[1,64]{1,0:T(1,128)} %param.13) | copy-start | bytes 772
  0.6 3.4 %copy-start.4 = (s32[2,128]{1,0:T(2,128)S(1)}, s32[2,128]{1,0:T(2,128)}, u32[]{:S(2)}) copy-start(s32[2,128]{1,0:T(2,128)} %constant.108.clone.1) | copy-start | bytes 3076
  0.7 3.6 %copy-start.3 = (bf16[256,128]{1,0:T(8,128)(2,1)S(1)}, bf16[256,128]{1,0:T(8,128)(2,1)}, u32[]{:S(2)}) copy-start(bf16[256,128]{1,0:T(8,128)(2,1)} %param.10) | copy-start | bytes 196612
  0.7 36.5 %copy-start.1 = (bf16[32,256]{1,0:T(8,128)(2,1)S(1)}, bf16[32,256]{1,0:T(8,128)(2,1)}, u32[]{:S(2)}) copy-start(bf16[32,256]{1,0:T(8,128)(2,1)} %param.9) | copy-start | bytes 49156
  2.2 40.6 %copy-start.5 = (s32[256]{0:T(256)S(1)}, s32[256]{0:T(256)}, u32[]{:S(2)}) copy-start(s32[256]{0:T(256)} %param.11) | copy-start | bytes 3076
  38.2 19.8 %all-to-all-start.1 = ((bf16[64,4,256]{2,1,0:T(4,128)(2,1)}), bf16[64,4,256]{2,1,0:T(4,128)(2,1)S(1)}, u32[]{:S(2)}, u32[]{:S(2)}) async-start(bf16[64,4,256]{2,1,0:T(4,128)(2,1)} %copy.38), calls=%async_computation.1 | async-start | bytes 262144 | tf_op jit(solution)/shard_map/all_to_all | solution.py:52
  61.4 22.9 %all-to-all-start.2 = ((f32[64,4,256]{2,1,0:T(4,128)}), f32[64,4,256]{2,1,0:T(4,128)S(1)}, u32[]{:S(2)}, u32[]{:S(2)}) async-start(f32[64,4,256]{2,1,0:T(4,128)} %copy.40), calls=%async_computation.2 | async-start | bytes 524288 | tf_op jit(solution)/shard_map/all_to_all | solution.py:69
  66.4 41.2 %copy-start.6 = (bf16[2048,256]{1,0:T(8,128)(2,1)S(1)}, bf16[2048,256]{1,0:T(8,128)(2,1)}, u32[]{:S(2)}) copy-start(bf16[2048,256]{1,0:T(8,128)(2,1)} %param.8) | copy-start | bytes 3145732
  84.6 24.6 %copy-start.2 = (bf16[32,256]{1,0:T(8,128)(2,1)}, bf16[32,256]{1,0:T(8,128)(2,1)S(1)}, u32[]{:S(2)}) copy-start(bf16[32,256]{1,0:T(8,128)(2,1)S(1)} %fusion.5) | copy-start | bytes 49156

commit v4 on v3

--- a/solution.py
+++ b/solution.py
@@ -14,24 +14,20 @@
     neur_local = traces.shape[0]
     frames = traces.shape[1]
     block_count = movie.shape[0] // BLOCK
-    slot_index = jnp.arange(slot_total, dtype=jnp.int32)
-    bucket_of = slot_index // capacity
-    position = slot_index % capacity
-    fill_slot = jnp.repeat(bucket_fill[0], capacity, total_repeat_length=slot_total)
-    usable = position < fill_slot
-    masked = footprints * usable[:, None].astype(jnp.bfloat16)
+    usable_op = jnp.arange(capacity, dtype=jnp.int32)[None, :] < bucket_fill[0][:, None]
+    masked_op = footprints.reshape(pix_count, capacity, BLOCK) * usable_op[:, :, None].astype(
+        jnp.bfloat16
+    )
+    power_op = jnp.sum(masked_op.astype(jnp.float32) ** 2, axis=2)
+    usable = usable_op.reshape(slot_total)
+    masked = masked_op.reshape(slot_total, BLOCK)
     block_pick = slot_block[:, None] == jnp.arange(block_count, dtype=jnp.int32)[None, :]
     dense_map = (block_pick.astype(jnp.bfloat16)[:, :, None] * masked[:, None, :]).reshape(
         slot_total, block_count * BLOCK
     )
-    slot_power = jnp.sum(masked.astype(jnp.float32) ** 2, axis=1)
     asked_and_power = lax.all_to_all(
         jnp.concatenate(
-            [
-                slot_neuron.astype(jnp.float32).reshape(pix_count, capacity),
-                slot_power.reshape(pix_count, capacity),
-            ],
-            axis=1,
+            [slot_neuron.reshape(pix_count, capacity).astype(jnp.float32), power_op], axis=1
         ),
         "pix",
         split_axis=0,

time: 136 us -> 133 us (0.978)
  local copies, waits for them, and re-layouts: 4.98 us -> 3.2 us
  matrix products: 7.09 us -> 5.42 us
    gather x1 -> x0, local copies, waits for them, and re-layouts: 1.87 us -> none  [local(): jnp.repeat(bucket_fill[0], capacity, total_repeat_length=slot_total)]
    dot_general x1, matrix products: 2.24 us -> 0.77 us  [local(): lax.dot_general(slot_updated, residual_two, (((1,), (1,)), ((), ())), pre...]
where the time goes in v4:
time: 133 us
  blocking collectives  77.7 us (58%)
  waiting for transfers between devices  31.5 us (24%)
  starting transfers between devices  9.66 us (7%)
  matrix products  5.42 us (4%)
  other arithmetic  4.24 us (3%)
  local copies, waits for them, and re-layouts  3.2 us (2%)
    all_to_all x1, blocking collectives, local(): lax.all_to_all(jnp.concatenate([slot_neuron.reshape(pix_count, capacity)....  32.4 us
    all_to_all x1, blocking collectives, slot_rows(): got = lax.all_to_all(picked, 'pix', split_axis=0, concat_axis=0, tiled=True)  22.3 us
    all_to_all x1, waiting for transfers between devices, local(): lax.all_to_all(projection, 'pix', split_axis=0, concat_axis=0, tiled=True)  17.5 us
    all_to_all x1, blocking collectives, local(): lax.all_to_all(stacked.reshape(tm_count, chunk, BLOCK), 'tm', split_axis=...  14.2 us
    all_to_all x1, waiting for transfers between devices, slot_rows(): got = lax.all_to_all(picked, 'pix', split_axis=0, concat_axis=0, tiled=True)  14 us
    all_to_all x1, blocking collectives, local(): lax.all_to_all(jnp.broadcast_to(mine, (tm_count, chunk, BLOCK)), 'tm', sp...  8.85 us
    all_to_all x1, starting transfers between devices, local(): lax.all_to_all(projection, 'pix', split_axis=0, concat_axis=0, tiled=True)  5.04 us
    all_to_all x1, starting transfers between devices, slot_rows(): got = lax.all_to_all(picked, 'pix', split_axis=0, concat_axis=0, tiled=True)  4.62 us
  transfers between devices with their start and end apart: 2, of which 2 were waited for; matrix products, arithmetic and copies ran while one was open for 1% of the time, Pallas kernels for 0%

profile of v4, /device:TPU:1, one launch (start us, length us, event | category | flops | bytes accessed | tf_op | source)
XLA Modules:
  0.0 132.6 jit_solution(14872494502167191244)
XLA Ops:
  0.6 0.7 convert_element_type.60
  1.3 0.7 iota_compare_fusion.4
  2.3 1.0 fusion.16
  3.5 32.4 %all_to_all.37 = f32[64,1,8]{2,1,0:T(1,128)S(1)} all-to-all(f32[64,1,8]{2,1,0:T(1,128)S(1)} %bitcast.39), channel_id=1, replica_groups=mesh['pix'=64,'tm'=8] {'pix'}, dimensions={0} | all-to-all | bytes 4096 | tf_op jit(solution)/shard_map/all_to_all | solution.py:28
  36.0 1.0 convolution_convert_fusion.1
  37.0 0.8 copy.38
  37.8 4.6 %all-to-all-start.1 = ((bf16[64,4,256]{2,1,0:T(4,128)(2,1)}), bf16[64,4,256]{2,1,0:T(4,128)(2,1)S(1)}, u32[]{:S(2)}, u32[]{:S(2)}) async-start(bf16[64,4,256]{2,1,0:T(4,128)(2,1)} %copy.38), calls=%async_computation.1 | async-start | bytes 262144 | tf_op jit(solution)/shard_map/all_to_all | solution.py:48
  42.4 0.1 copy.36
  42.5 0.7 broadcast_multiply_fusion
  43.2 0.3 mul.48
  43.5 14.0 %all-to-all-done.1 = bf16[64,4,256]{2,1,0:T(4,128)(2,1)S(1)} async-done(((bf16[64,4,256]{2,1,0:T(4,128)(2,1)}), bf16[64,4,256]{2,1,0:T(4,128)(2,1)S(1)}, u32[]{:S(2)}, u32[]{:S(2)}) %all-to-all-start.1) | async-done | bytes 131104 | tf_op jit(solution)/shard_map/all_to_all | solution.py:48
  57.6 2.5 %fusion.9 = f32[64,4,256]{2,0,1:T(8,128)S(1)} fusion(bf16[64,4,2048]{2,1,0:T(4,128)(2,1)S(1)} %mul.48, bf16[256,256]{1,0:T(8,128)(2,1)S(1)} %reshape.151, bf16[2048,256]{1,0:T(8,128)(2,1)} %param.6, bf16[32,8,16,128]{3,2,1,0:T(8,128)(2,1)S(1)} %bitcast.36), kind=kOutput, calls=%fused_computation.16 | convolution fusion | flops 538443776 | bytes 3538944 | tf_op jit(solution)/shard_map/okp,pf->okf/dot_general | solution.py:59
  60.1 0.9 copy.40
  61.0 5.0 %all-to-all-start.2 = ((f32[64,4,256]{2,1,0:T(4,128)}), f32[64,4,256]{2,1,0:T(4,128)S(1)}, u32[]{:S(2)}, u32[]{:S(2)}) async-start(f32[64,4,256]{2,1,0:T(4,128)} %copy.40), calls=%async_computation.2 | async-start | bytes 524288 | tf_op jit(solution)/shard_map/all_to_all | solution.py:65
  66.3 0.1 fusion.6
  66.4 17.5 %all-to-all-done.2 = f32[64,4,256]{2,1,0:T(4,128)S(1)} async-done(((f32[64,4,256]{2,1,0:T(4,128)}), f32[64,4,256]{2,1,0:T(4,128)S(1)}, u32[]{:S(2)}, u32[]{:S(2)}) %all-to-all-start.2) | async-done | bytes 262176 | tf_op jit(solution)/shard_map/all_to_all | solution.py:65
  84.1 0.2 fusion.5
  84.3 0.2 convolution_convert_fusion
  84.6 22.3 %all_to_all.38 = bf16[64,4,256]{2,1,0:T(4,128)(2,1)S(1)} all-to-all(bf16[64,4,256]{2,1,0:T(4,128)(2,1)S(1)} %copy.41), channel_id=1, replica_groups=mesh['pix'=64,'tm'=8] {'pix'}, dimensions={0} | all-to-all | bytes 262144 | tf_op jit(solution)/shard_map/all_to_all | solution.py:48
  107.3 0.6 fusion.1
  107.9 0.8 select_reduce_fusion
  108.8 14.2 %all_to_all.39 = f32[8,33,128]{2,1,0:T(8,128)S(1)} all-to-all(f32[8,33,128]{2,1,0:T(8,128)S(1)} %reshape.156), channel_id=1, replica_groups=mesh['pix'=64,'tm'=8] {'tm'}, dimensions={0} | all-to-all | bytes 270336 | tf_op jit(solution)/shard_map/all_to_all | solution.py:88
  123.0 8.8 %all_to_all.40 = f32[8,33,128]{2,1,0:T(8,128)S(1)} all-to-all(f32[8,33,128]{2,1,0:T(8,128)S(1)} %broadcast_in_dim.23), channel_id=1, replica_groups=mesh['pix'=64,'tm'=8] {'tm'}, dimensions={0} | all-to-all | bytes 270336 | tf_op jit(solution)/shard_map/all_to_all | solution.py:92
  131.9 0.8 fusion.18
  (32 shorter events, 1.5 us)
Async XLA Ops:
  0.6 41.8 %copy-start.2 = (s32[256]{0:T(256)S(1)}, s32[256]{0:T(256)}, u32[]{:S(2)}) copy-start(s32[256]{0:T(256)} %param.9) | copy-start | bytes 3076
  37.8 19.8 %all-to-all-start.1 = ((bf16[64,4,256]{2,1,0:T(4,128)(2,1)}), bf16[64,4,256]{2,1,0:T(4,128)(2,1)S(1)}, u32[]{:S(2)}, u32[]{:S(2)}) async-start(bf16[64,4,256]{2,1,0:T(4,128)(2,1)} %copy.38), calls=%async_computation.1 | async-start | bytes 262144 | tf_op jit(solution)/shard_map/all_to_all | solution.py:48
  60.1 23.9 %copy-start = (bf16[32,256]{1,0:T(8,128)(2,1)S(1)}, bf16[32,256]{1,0:T(8,128)(2,1)}, u32[]{:S(2)}) copy-start(bf16[32,256]{1,0:T(8,128)(2,1)} %param.7) | copy-start | bytes 49156
  61.0 22.9 %all-to-all-start.2 = ((f32[64,4,256]{2,1,0:T(4,128)}), f32[64,4,256]{2,1,0:T(4,128)S(1)}, u32[]{:S(2)}, u32[]{:S(2)}) async-start(f32[64,4,256]{2,1,0:T(4,128)} %copy.40), calls=%async_computation.2 | async-start | bytes 524288 | tf_op jit(solution)/shard_map/all_to_all | solution.py:65
  66.0 41.3 %copy-start.3 = (bf16[2048,256]{1,0:T(8,128)(2,1)S(1)}, bf16[2048,256]{1,0:T(8,128)(2,1)}, u32[]{:S(2)}) copy-start(bf16[2048,256]{1,0:T(8,128)(2,1)} %param.6) | copy-start | bytes 3145732
  84.3 23.6 %copy-start.1 = (bf16[32,256]{1,0:T(8,128)(2,1)}, bf16[32,256]{1,0:T(8,128)(2,1)S(1)}, u32[]{:S(2)}) copy-start(bf16[32,256]{1,0:T(8,128)(2,1)S(1)} %fusion.5) | copy-start | bytes 49156

commit v5 on v4

--- a/solution.py
+++ b/solution.py
@@ -18,7 +18,11 @@
     masked_op = footprints.reshape(pix_count, capacity, BLOCK) * usable_op[:, :, None].astype(
         jnp.bfloat16
     )
-    power_op = jnp.sum(masked_op.astype(jnp.float32) ** 2, axis=2)
+    power_op = jnp.where(
+        usable_op,
+        jnp.sum(footprints.reshape(pix_count, capacity, BLOCK).astype(jnp.float32) ** 2, axis=2),
+        0.0,
+    )
     usable = usable_op.reshape(slot_total)
     masked = masked_op.reshape(slot_total, BLOCK)
     block_pick = slot_block[:, None] == jnp.arange(block_count, dtype=jnp.int32)[None, :]

time: 133 us -> 134 us (level)
  blocking collectives: 77.7 us -> 45.1 us
  starting transfers between devices: 9.66 us -> 28.8 us
  waiting for transfers between devices: 31.5 us -> 44 us
  other arithmetic: 4.24 us -> 5.72 us
    all_to_all x1 -> x0, blocking collectives: 32.4 us -> none  [local(): lax.all_to_all(jnp.concatenate([slot_neuron.reshape(pix_count, capacity)....]
    all_to_all x0 -> x1, starting transfers between devices: none -> 19.1 us  [local(): lax.all_to_all(jnp.concatenate([slot_neuron.reshape(pix_count, capacity)....]
    all_to_all x0 -> x1, waiting for transfers between devices: none -> 12.7 us  [local(): lax.all_to_all(jnp.concatenate([slot_neuron.reshape(pix_count, capacity)....]
  transfers between devices with their start and end apart: 2 -> 3, of which waited for: 2 -> 3; matrix products, arithmetic and copies ran while one was open for 1% -> 2% of each run, Pallas kernels for 0% -> 0%
where the time goes in v5:
time: 134 us; the launch traced here: 133 us
  blocking collectives  45.1 us (34%)
  waiting for transfers between devices  44 us (33%)
  starting transfers between devices  28.8 us (21%)
  other arithmetic  5.72 us (4%)
  matrix products  5.38 us (4%)
  local copies, waits for them, and re-layouts  3.2 us (2%)
    all_to_all x1, blocking collectives, slot_rows(): got = lax.all_to_all(picked, 'pix', split_axis=0, concat_axis=0, tiled=True)  22.3 us
    all_to_all x1, starting transfers between devices, local(): lax.all_to_all(jnp.concatenate([slot_neuron.reshape(pix_count, capacity)....  19.1 us
    all_to_all x1, waiting for transfers between devices, local(): lax.all_to_all(projection, 'pix', split_axis=0, concat_axis=0, tiled=True)  17.5 us
    all_to_all x1, blocking collectives, local(): lax.all_to_all(stacked.reshape(tm_count, chunk, BLOCK), 'tm', split_axis=...  14 us
    all_to_all x1, waiting for transfers between devices, slot_rows(): got = lax.all_to_all(picked, 'pix', split_axis=0, concat_axis=0, tiled=True)  13.7 us
    all_to_all x1, waiting for transfers between devices, local(): lax.all_to_all(jnp.concatenate([slot_neuron.reshape(pix_count, capacity)....  12.7 us
    all_to_all x1, blocking collectives, local(): lax.all_to_all(jnp.broadcast_to(mine, (tm_count, chunk, BLOCK)), 'tm', sp...  8.85 us
    all_to_all x1, starting transfers between devices, local(): lax.all_to_all(projection, 'pix', split_axis=0, concat_axis=0, tiled=True)  5.04 us
  transfers between devices with their start and end apart: 3, of which 3 were waited for; matrix products, arithmetic and copies ran while one was open for 2% of the time, Pallas kernels for 0%

profile of v5, /device:TPU:1, one launch (start us, length us, event | category | flops | bytes accessed | tf_op | source)
XLA Modules:
  0.0 133.1 jit_solution(10528118798640562552)
XLA Ops:
  0.7 0.7 convert_element_type.62
  1.4 0.9 multiply_reduce_fusion.1
  2.5 0.7 broadcast_select_fusion
  3.3 0.7 pad_maximum_fusion
  4.0 19.1 %all-to-all-start = ((f32[64,1,8]{2,1,0:T(1,128)}), f32[64,1,8]{2,1,0:T(1,128)S(1)}, u32[]{:S(2)}, u32[]{:S(2)}) async-start(f32[64,1,8]{2,1,0:T(1,128)} %bitcast.2), calls=%async_computation | async-start | bytes 65536 | tf_op jit(solution)/shard_map/all_to_all | solution.py:32
  23.1 0.7 iota_compare_fusion.8
  23.8 12.7 %all-to-all-done = f32[64,1,8]{2,1,0:T(1,128)S(1)} async-done(((f32[64,1,8]{2,1,0:T(1,128)}), f32[64,1,8]{2,1,0:T(1,128)S(1)}, u32[]{:S(2)}, u32[]{:S(2)}) %all-to-all-start) | async-done | bytes 2080 | tf_op jit(solution)/shard_map/all_to_all | solution.py:32
  36.6 1.0 convolution_convert_fusion.1
  37.6 0.8 copy.38
  38.4 4.6 %all-to-all-start.1 = ((bf16[64,4,256]{2,1,0:T(4,128)(2,1)}), bf16[64,4,256]{2,1,0:T(4,128)(2,1)S(1)}, u32[]{:S(2)}, u32[]{:S(2)}) async-start(bf16[64,4,256]{2,1,0:T(4,128)(2,1)} %copy.38), calls=%async_computation.1 | async-start | bytes 262144 | tf_op jit(solution)/shard_map/all_to_all | solution.py:52
  43.4 0.7 broadcast_multiply_fusion
  44.2 0.3 mul.47
  44.4 13.7 %all-to-all-done.1 = bf16[64,4,256]{2,1,0:T(4,128)(2,1)S(1)} async-done(((bf16[64,4,256]{2,1,0:T(4,128)(2,1)}), bf16[64,4,256]{2,1,0:T(4,128)(2,1)S(1)}, u32[]{:S(2)}, u32[]{:S(2)}) %all-to-all-start.1) | async-done | bytes 131104 | tf_op jit(solution)/shard_map/all_to_all | solution.py:52
  58.2 2.5 %fusion.9 = f32[64,4,256]{2,0,1:T(8,128)S(1)} fusion(bf16[64,4,2048]{2,1,0:T(4,128)(2,1)S(1)} %mul.47, bf16[256,256]{1,0:T(8,128)(2,1)S(1)} %reshape.150, bf16[2048,256]{1,0:T(8,128)(2,1)} %param.6, bf16[32,8,16,128]{3,2,1,0:T(8,128)(2,1)S(1)} %bitcast.36), kind=kOutput, calls=%fused_computation.16 | convolution fusion | flops 538443776 | bytes 3538944 | tf_op jit(solution)/shard_map/okp,pf->okf/dot_general | solution.py:63
  60.7 0.9 copy.40
  61.6 5.0 %all-to-all-start.2 = ((f32[64,4,256]{2,1,0:T(4,128)}), f32[64,4,256]{2,1,0:T(4,128)S(1)}, u32[]{:S(2)}, u32[]{:S(2)}) async-start(f32[64,4,256]{2,1,0:T(4,128)} %copy.40), calls=%async_computation.2 | async-start | bytes 524288 | tf_op jit(solution)/shard_map/all_to_all | solution.py:69
  67.0 17.5 %all-to-all-done.2 = f32[64,4,256]{2,1,0:T(4,128)S(1)} async-done(((f32[64,4,256]{2,1,0:T(4,128)}), f32[64,4,256]{2,1,0:T(4,128)S(1)}, u32[]{:S(2)}, u32[]{:S(2)}) %all-to-all-start.2) | async-done | bytes 262176 | tf_op jit(solution)/shard_map/all_to_all | solution.py:69
  84.6 0.2 fusion.5
  85.2 22.3 %all_to_all.37 = bf16[64,4,256]{2,1,0:T(4,128)(2,1)S(1)} all-to-all(bf16[64,4,256]{2,1,0:T(4,128)(2,1)S(1)} %copy.41), channel_id=1, replica_groups=mesh['pix'=64,'tm'=8] {'pix'}, dimensions={0} | all-to-all | bytes 262144 | tf_op jit(solution)/shard_map/all_to_all | solution.py:52
  107.9 0.6 fusion.1
  108.5 0.8 select_reduce_fusion
  109.4 14.0 %all_to_all.38 = f32[8,33,128]{2,1,0:T(8,128)S(1)} all-to-all(f32[8,33,128]{2,1,0:T(8,128)S(1)} %reshape.155), channel_id=1, replica_groups=mesh['pix'=64,'tm'=8] {'tm'}, dimensions={0} | all-to-all | bytes 270336 | tf_op jit(solution)/shard_map/all_to_all | solution.py:92
  123.4 8.8 %all_to_all.39 = f32[8,33,128]{2,1,0:T(8,128)S(1)} all-to-all(f32[8,33,128]{2,1,0:T(8,128)S(1)} %broadcast_in_dim.28), channel_id=1, replica_groups=mesh['pix'=64,'tm'=8] {'tm'}, dimensions={0} | all-to-all | bytes 270336 | tf_op jit(solution)/shard_map/all_to_all | solution.py:96
  132.2 0.8 fusion.18
  (37 shorter events, 2.0 us)
Async XLA Ops:
  0.6 42.7 %copy-start = (bf16[256,128]{1,0:T(8,128)(2,1)S(1)}, bf16[256,128]{1,0:T(8,128)(2,1)}, u32[]{:S(2)}) copy-start(bf16[256,128]{1,0:T(8,128)(2,1)} %param.8) | copy-start | bytes 196612
  0.6 42.3 %copy-start.3 = (s32[1,64]{1,0:T(1,128)S(1)}, s32[1,64]{1,0:T(1,128)}, u32[]{:S(2)}) copy-start(s32[1,64]{1,0:T(1,128)} %param.11) | copy-start | bytes 772
  4.0 32.5 %all-to-all-start = ((f32[64,1,8]{2,1,0:T(1,128)}), f32[64,1,8]{2,1,0:T(1,128)S(1)}, u32[]{:S(2)}, u32[]{:S(2)}) async-start(f32[64,1,8]{2,1,0:T(1,128)} %bitcast.2), calls=%async_computation | async-start | bytes 65536 | tf_op jit(solution)/shard_map/all_to_all | solution.py:32
  38.4 19.8 %all-to-all-start.1 = ((bf16[64,4,256]{2,1,0:T(4,128)(2,1)}), bf16[64,4,256]{2,1,0:T(4,128)(2,1)S(1)}, u32[]{:S(2)}, u32[]{:S(2)}) async-start(bf16[64,4,256]{2,1,0:T(4,128)(2,1)} %copy.38), calls=%async_computation.1 | async-start | bytes 262144 | tf_op jit(solution)/shard_map/all_to_all | solution.py:52
  60.7 23.9 %copy-start.1 = (bf16[32,256]{1,0:T(8,128)(2,1)S(1)}, bf16[32,256]{1,0:T(8,128)(2,1)}, u32[]{:S(2)}) copy-start(bf16[32,256]{1,0:T(8,128)(2,1)} %param.7) | copy-start | bytes 49156
  61.6 22.9 %all-to-all-start.2 = ((f32[64,4,256]{2,1,0:T(4,128)}), f32[64,4,256]{2,1,0:T(4,128)S(1)}, u32[]{:S(2)}, u32[]{:S(2)}) async-start(f32[64,4,256]{2,1,0:T(4,128)} %copy.40), calls=%async_computation.2 | async-start | bytes 524288 | tf_op jit(solution)/shard_map/all_to_all | solution.py:69
  66.6 41.3 %copy-start.4 = (bf16[2048,256]{1,0:T(8,128)(2,1)S(1)}, bf16[2048,256]{1,0:T(8,128)(2,1)}, u32[]{:S(2)}) copy-start(bf16[2048,256]{1,0:T(8,128)(2,1)} %param.6) | copy-start | bytes 3145732
  84.8 23.6 %copy-start.2 = (bf16[32,256]{1,0:T(8,128)(2,1)}, bf16[32,256]{1,0:T(8,128)(2,1)S(1)}, u32[]{:S(2)}) copy-start(bf16[32,256]{1,0:T(8,128)(2,1)S(1)} %fusion.5) | copy-start | bytes 49156

commit v6 on v4

--- a/solution.py
+++ b/solution.py
@@ -80,22 +80,27 @@
     ).reshape(slot_total, block_count, BLOCK)
     numerator = jnp.sum(jnp.where(block_pick[:, :, None], products, 0.0), axis=1)
     trace_power = jnp.sum(slot_updated.astype(jnp.float32) ** 2, axis=1)
-    pl_rows = slot_total // BLOCK
-    stacked = jnp.concatenate([numerator, trace_power.reshape(pl_rows, BLOCK)], axis=0)
-    rows = stacked.shape[0]
-    chunk = -(-rows // tm_count)
-    stacked = jnp.pad(stacked, ((0, chunk * tm_count - rows), (0, 0)))
-    parts = lax.all_to_all(
-        stacked.reshape(tm_count, chunk, BLOCK), "tm", split_axis=0, concat_axis=0, tiled=True
+    per = slot_total // tm_count
+    stacked = jnp.concatenate(
+        [
+            numerator.reshape(tm_count, per, BLOCK),
+            jnp.pad(trace_power.reshape(tm_count, 1, per), ((0, 0), (0, 0), (0, BLOCK - per))),
+        ],
+        axis=1,
     )
-    mine = jnp.sum(parts, axis=0, keepdims=True)
+    parts = lax.all_to_all(stacked, "tm", split_axis=0, concat_axis=0, tiled=True)
+    mine = jnp.sum(parts, axis=0)
+    first = lax.axis_index("tm") * per
+    masked_mine = lax.dynamic_slice_in_dim(masked, first, per, 0)
+    usable_mine = lax.dynamic_slice_in_dim(usable, first, per, 0)
+    grown = jnp.maximum(
+        0.0, masked_mine.astype(jnp.float32) + mine[:per] / (mine[per, :per] + 1e-06)[:, None]
+    )
+    grown = jnp.where(usable_mine[:, None], grown, 0.0)
     whole = lax.all_to_all(
-        jnp.broadcast_to(mine, (tm_count, chunk, BLOCK)), "tm", split_axis=0, concat_axis=0, tiled=True
-    ).reshape(chunk * tm_count, BLOCK)
-    numer_all = whole[:slot_total]
-    power_all = whole[slot_total : slot_total + pl_rows].reshape(slot_total)
-    grown = jnp.maximum(0.0, masked.astype(jnp.float32) + numer_all / (power_all + 1e-06)[:, None])
-    return (updated, jnp.where(usable[:, None], grown, 0.0))
+        jnp.broadcast_to(grown[None], (tm_count, per, BLOCK)), "tm", split_axis=0, concat_axis=0, tiled=True
+    ).reshape(slot_total, BLOCK)
+    return (updated, whole)
 
 
 def solution(mesh):

time: 133 us -> 133 us (level)
  blocking collectives: 77.7 us -> 63.3 us
  starting transfers between devices: 9.66 us -> 18.3 us
  waiting for transfers between devices: 31.5 us -> 37 us
    all_to_all x2 -> x1, blocking collectives: 23 us -> 8.53 us  [local(): lax.all_to_all(jnp.broadcast_to(grown[None], (tm_count, per, BLOCK)), 'tm...]
    all_to_all x0 -> x1, starting transfers between devices: none -> 8.61 us  [local(): lax.all_to_all(stacked, 'tm', split_axis=0, concat_axis=0, tiled=True)]
    all_to_all x0 -> x1, waiting for transfers between devices: none -> 5.47 us  [local(): lax.all_to_all(stacked, 'tm', split_axis=0, concat_axis=0, tiled=True)]
  transfers between devices with their start and end apart: 2 -> 3, of which waited for: 2 -> 3; matrix products, arithmetic and copies ran while one was open for 1% -> 1% of each run, Pallas kernels for 0% -> 0%
where the time goes in v6:
time: 133 us
  blocking collectives  63.3 us (48%)
  waiting for transfers between devices  37 us (28%)
  starting transfers between devices  18.3 us (14%)
  matrix products  5.42 us (4%)
  other arithmetic  4.19 us (3%)
  local copies, waits for them, and re-layouts  3.87 us (3%)
    all_to_all x1, blocking collectives, local(): lax.all_to_all(jnp.concatenate([slot_neuron.reshape(pix_count, capacity)....  32.4 us
    all_to_all x1, blocking collectives, slot_rows(): got = lax.all_to_all(picked, 'pix', split_axis=0, concat_axis=0, tiled=True)  22.3 us
    all_to_all x1, waiting for transfers between devices, local(): lax.all_to_all(projection, 'pix', split_axis=0, concat_axis=0, tiled=True)  17.5 us
    all_to_all x1, waiting for transfers between devices, slot_rows(): got = lax.all_to_all(picked, 'pix', split_axis=0, concat_axis=0, tiled=True)  14 us
    all_to_all x1, starting transfers between devices, local(): lax.all_to_all(stacked, 'tm', split_axis=0, concat_axis=0, tiled=True)  8.61 us
    all_to_all x1, blocking collectives, local(): lax.all_to_all(jnp.broadcast_to(grown[None], (tm_count, per, BLOCK)), 'tm...  8.53 us
    all_to_all x1, waiting for transfers between devices, local(): lax.all_to_all(stacked, 'tm', split_axis=0, concat_axis=0, tiled=True)  5.47 us
    all_to_all x1, starting transfers between devices, local(): lax.all_to_all(projection, 'pix', split_axis=0, concat_axis=0, tiled=True)  5.04 us
  transfers between devices with their start and end apart: 3, of which 3 were waited for; matrix products, arithmetic and copies ran while one was open for 1% of the time, Pallas kernels for 0%

profile of v6, /device:TPU:1, one launch (start us, length us, event | category | flops | bytes accessed | tf_op | source)
XLA Modules:
  0.0 132.9 jit_solution(5001478170153642695)
XLA Ops:
  0.6 0.7 convert_element_type.62
  1.3 0.7 iota_compare_fusion.4
  2.3 1.0 multiply_reduce_fusion.1
  3.5 32.4 %all_to_all.37 = f32[64,1,8]{2,1,0:T(1,128)S(1)} all-to-all(f32[64,1,8]{2,1,0:T(1,128)S(1)} %bitcast.44), channel_id=1, replica_groups=mesh['pix'=64,'tm'=8] {'pix'}, dimensions={0} | all-to-all | bytes 4096 | tf_op jit(solution)/shard_map/all_to_all | solution.py:28
  36.0 1.0 convolution_convert_fusion.1
  37.0 0.8 copy.51
  37.8 4.6 %all-to-all-start.1 = ((bf16[64,4,256]{2,1,0:T(4,128)(2,1)}), bf16[64,4,256]{2,1,0:T(4,128)(2,1)S(1)}, u32[]{:S(2)}, u32[]{:S(2)}) async-start(bf16[64,4,256]{2,1,0:T(4,128)(2,1)} %copy.51), calls=%async_computation.1 | async-start | bytes 262144 | tf_op jit(solution)/shard_map/all_to_all | solution.py:48
  42.5 0.7 broadcast_multiply_fusion
  43.2 0.3 mul.51
  43.5 14.0 %all-to-all-done.1 = bf16[64,4,256]{2,1,0:T(4,128)(2,1)S(1)} async-done(((bf16[64,4,256]{2,1,0:T(4,128)(2,1)}), bf16[64,4,256]{2,1,0:T(4,128)(2,1)S(1)}, u32[]{:S(2)}, u32[]{:S(2)}) %all-to-all-start.1) | async-done | bytes 131104 | tf_op jit(solution)/shard_map/all_to_all | solution.py:48
  57.6 2.5 %fusion.9 = f32[64,4,256]{2,0,1:T(8,128)S(1)} fusion(bf16[64,4,2048]{2,1,0:T(4,128)(2,1)S(1)} %mul.51, bf16[256,256]{1,0:T(8,128)(2,1)S(1)} %reshape.141, bf16[2048,256]{1,0:T(8,128)(2,1)} %param.6, bf16[32,8,16,128]{3,2,1,0:T(8,128)(2,1)S(1)} %bitcast.39), kind=kOutput, calls=%fused_computation.16 | convolution fusion | flops 538443776 | bytes 3538944 | tf_op jit(solution)/shard_map/okp,pf->okf/dot_general | solution.py:59
  60.1 0.9 copy.53
  61.0 5.0 %all-to-all-start.2 = ((f32[64,4,256]{2,1,0:T(4,128)}), f32[64,4,256]{2,1,0:T(4,128)S(1)}, u32[]{:S(2)}, u32[]{:S(2)}) async-start(f32[64,4,256]{2,1,0:T(4,128)} %copy.53), calls=%async_computation.2 | async-start | bytes 524288 | tf_op jit(solution)/shard_map/all_to_all | solution.py:65
  66.4 17.5 %all-to-all-done.2 = f32[64,4,256]{2,1,0:T(4,128)S(1)} async-done(((f32[64,4,256]{2,1,0:T(4,128)}), f32[64,4,256]{2,1,0:T(4,128)S(1)}, u32[]{:S(2)}, u32[]{:S(2)}) %all-to-all-start.2) | async-done | bytes 262176 | tf_op jit(solution)/shard_map/all_to_all | solution.py:65
  84.0 0.2 fusion.5
  84.3 0.2 convolution_convert_fusion
  84.6 22.3 %all_to_all.38 = bf16[64,4,256]{2,1,0:T(4,128)(2,1)S(1)} all-to-all(bf16[64,4,256]{2,1,0:T(4,128)(2,1)S(1)} %copy.54), channel_id=1, replica_groups=mesh['pix'=64,'tm'=8] {'pix'}, dimensions={0} | all-to-all | bytes 262144 | tf_op jit(solution)/shard_map/all_to_all | solution.py:48
  107.3 0.6 fusion.1
  107.9 0.8 select_reduce_fusion
  108.7 0.7 select_maximum_fusion
  109.4 8.6 %all-to-all-start.4 = ((f32[8,33,128]{2,1,0:T(8,128)}), f32[8,33,128]{2,1,0:T(8,128)S(1)}, u32[]{:S(2)}, u32[]{:S(2)}) async-start(f32[8,33,128]{2,1,0:T(8,128)} %select_maximum_fusion), calls=%async_computation.4 | async-start | bytes 327680 | tf_op jit(solution)/shard_map/all_to_all | solution.py:91
  118.1 5.5 %all-to-all-done.4 = f32[8,33,128]{2,1,0:T(8,128)S(1)} async-done(((f32[8,33,128]{2,1,0:T(8,128)}), f32[8,33,128]{2,1,0:T(8,128)S(1)}, u32[]{:S(2)}, u32[]{:S(2)}) %all-to-all-start.4) | async-done | bytes 135200 | tf_op jit(solution)/shard_map/all_to_all | solution.py:91
  123.7 8.5 %all_to_all.39 = f32[8,32,128]{2,1,0:T(8,128)S(1)} all-to-all(f32[8,32,128]{2,1,0:T(8,128)S(1)} %broadcast_in_dim.23), channel_id=1, replica_groups=mesh['pix'=64,'tm'=8] {'tm'}, dimensions={0} | all-to-all | bytes 262144 | tf_op jit(solution)/shard_map/all_to_all | solution.py:100
  132.2 0.7 copy.76
  (33 shorter events, 1.8 us)
Async XLA Ops:
  0.6 41.8 %copy-start.2 = (s32[256]{0:T(256)S(1)}, s32[256]{0:T(256)}, u32[]{:S(2)}) copy-start(s32[256]{0:T(256)} %param.9) | copy-start | bytes 3076
  37.8 19.8 %all-to-all-start.1 = ((bf16[64,4,256]{2,1,0:T(4,128)(2,1)}), bf16[64,4,256]{2,1,0:T(4,128)(2,1)S(1)}, u32[]{:S(2)}, u32[]{:S(2)}) async-start(bf16[64,4,256]{2,1,0:T(4,128)(2,1)} %copy.51), calls=%async_computation.1 | async-start | bytes 262144 | tf_op jit(solution)/shard_map/all_to_all | solution.py:48
  60.1 23.9 %copy-start = (bf16[32,256]{1,0:T(8,128)(2,1)S(1)}, bf16[32,256]{1,0:T(8,128)(2,1)}, u32[]{:S(2)}) copy-start(bf16[32,256]{1,0:T(8,128)(2,1)} %param.7) | copy-start | bytes 49156
  61.0 22.9 %all-to-all-start.2 = ((f32[64,4,256]{2,1,0:T(4,128)}), f32[64,4,256]{2,1,0:T(4,128)S(1)}, u32[]{:S(2)}, u32[]{:S(2)}) async-start(f32[64,4,256]{2,1,0:T(4,128)} %copy.53), calls=%async_computation.2 | async-start | bytes 524288 | tf_op jit(solution)/shard_map/all_to_all | solution.py:65
  66.0 41.3 %copy-start.3 = (bf16[2048,256]{1,0:T(8,128)(2,1)S(1)}, bf16[2048,256]{1,0:T(8,128)(2,1)}, u32[]{:S(2)}) copy-start(bf16[2048,256]{1,0:T(8,128)(2,1)} %param.6) | copy-start | bytes 3145732
  84.3 23.6 %copy-start.1 = (bf16[32,256]{1,0:T(8,128)(2,1)}, bf16[32,256]{1,0:T(8,128)(2,1)S(1)}, u32[]{:S(2)}) copy-start(bf16[32,256]{1,0:T(8,128)(2,1)S(1)} %fusion.5) | copy-start | bytes 49156
  109.4 14.2 %all-to-all-start.4 = ((f32[8,33,128]{2,1,0:T(8,128)}), f32[8,33,128]{2,1,0:T(8,128)S(1)}, u32[]{:S(2)}, u32[]{:S(2)}) async-start(f32[8,33,128]{2,1,0:T(8,128)} %select_maximum_fusion), calls=%async_computation.4 | async-start | bytes 327680 | tf_op jit(solution)/shard_map/all_to_all | solution.py:91

commit v7 on v6

--- a/solution.py
+++ b/solution.py
@@ -84,13 +84,22 @@
     stacked = jnp.concatenate(
         [
             numerator.reshape(tm_count, per, BLOCK),
-            jnp.pad(trace_power.reshape(tm_count, 1, per), ((0, 0), (0, 0), (0, BLOCK - per))),
+            jnp.concatenate(
+                [
+                    trace_power.reshape(tm_count, 1, per),
+                    jnp.broadcast_to(
+                        0.0 * trace_power[0], (tm_count, 1, BLOCK - per - 1)
+                    ),
+                    jnp.arange(tm_count, dtype=jnp.float32)[:, None, None] + 0.0 * trace_power[0],
+                ],
+                axis=2,
+            ),
         ],
         axis=1,
     )
     parts = lax.all_to_all(stacked, "tm", split_axis=0, concat_axis=0, tiled=True)
     mine = jnp.sum(parts, axis=0)
-    first = lax.axis_index("tm") * per
+    first = parts[0, per, BLOCK - 1].astype(jnp.int32) * per
     masked_mine = lax.dynamic_slice_in_dim(masked, first, per, 0)
     usable_mine = lax.dynamic_slice_in_dim(usable, first, per, 0)
     grown = jnp.maximum(

time: 133 us -> 136 us (1.023)
  blocking collectives: 63.3 us -> 77.4 us
  starting transfers between devices: 18.3 us -> 9.66 us
  waiting for transfers between devices: 37 us -> 31.5 us
    all_to_all x0 -> x1, blocking collectives: none -> 14.2 us  [local(): lax.all_to_all(stacked, 'tm', split_axis=0, concat_axis=0, tiled=True)]
    all_to_all x1 -> x0, starting transfers between devices: 8.61 us -> none  [local(): lax.all_to_all(stacked, 'tm', split_axis=0, concat_axis=0, tiled=True)]
    all_to_all x1 -> x0, waiting for transfers between devices: 5.47 us -> none  [local(): lax.all_to_all(stacked, 'tm', split_axis=0, concat_axis=0, tiled=True)]
  transfers between devices with their start and end apart: 3 -> 2, of which waited for: 3 -> 2; matrix products, arithmetic and copies ran while one was open for 1% -> 1% of each run, Pallas kernels for 0% -> 0%
where the time goes in v7:
time: 136 us; the launch traced here: 135 us
  blocking collectives  77.4 us (57%)
  waiting for transfers between devices  31.5 us (23%)
  starting transfers between devices  9.66 us (7%)
  matrix products  5.42 us (4%)
  local copies, waits for them, and re-layouts  5.16 us (4%)
  other arithmetic  3.61 us (3%)
  between operations  2.19 us (2%)
    all_to_all x1, blocking collectives, local(): lax.all_to_all(jnp.concatenate([slot_neuron.reshape(pix_count, capacity)....  32.4 us
    all_to_all x1, blocking collectives, slot_rows(): got = lax.all_to_all(picked, 'pix', split_axis=0, concat_axis=0, tiled=True)  22.3 us
    all_to_all x1, waiting for transfers between devices, local(): lax.all_to_all(projection, 'pix', split_axis=0, concat_axis=0, tiled=True)  17.5 us
    all_to_all x1, blocking collectives, local(): lax.all_to_all(stacked, 'tm', split_axis=0, concat_axis=0, tiled=True)  14.2 us
    all_to_all x1, waiting for transfers between devices, slot_rows(): got = lax.all_to_all(picked, 'pix', split_axis=0, concat_axis=0, tiled=True)  14 us
    all_to_all x1, blocking collectives, local(): lax.all_to_all(jnp.broadcast_to(grown[None], (tm_count, per, BLOCK)), 'tm...  8.53 us
    all_to_all x1, starting transfers between devices, local(): lax.all_to_all(projection, 'pix', split_axis=0, concat_axis=0, tiled=True)  5.04 us
    all_to_all x1, starting transfers between devices, slot_rows(): got = lax.all_to_all(picked, 'pix', split_axis=0, concat_axis=0, tiled=True)  4.62 us
  transfers between devices with their start and end apart: 2, of which 2 were waited for; matrix products, arithmetic and copies ran while one was open for 1% of the time, Pallas kernels for 0%

profile of v7, /device:TPU:1, one launch (start us, length us, event | category | flops | bytes accessed | tf_op | source)
XLA Modules:
  0.0 135.0 jit_solution(2587660012209637447)
XLA Ops:
  0.6 0.7 convert_element_type.64
  1.3 0.7 iota_compare_fusion.3
  2.3 1.0 multiply_reduce_fusion.1
  3.5 32.4 %all_to_all.37 = f32[64,1,8]{2,1,0:T(1,128)S(1)} all-to-all(f32[64,1,8]{2,1,0:T(1,128)S(1)} %bitcast.45), channel_id=1, replica_groups=mesh['pix'=64,'tm'=8] {'pix'}, dimensions={0} | all-to-all | bytes 4096 | tf_op jit(solution)/shard_map/all_to_all | solution.py:28
  36.0 1.0 convolution_convert_fusion.1
  37.0 0.8 copy.54
  37.8 4.6 %all-to-all-start.1 = ((bf16[64,4,256]{2,1,0:T(4,128)(2,1)}), bf16[64,4,256]{2,1,0:T(4,128)(2,1)S(1)}, u32[]{:S(2)}, u32[]{:S(2)}) async-start(bf16[64,4,256]{2,1,0:T(4,128)(2,1)} %copy.54), calls=%async_computation.1 | async-start | bytes 262144 | tf_op jit(solution)/shard_map/all_to_all | solution.py:48
  42.5 0.7 broadcast_multiply_fusion
  43.2 0.3 mul.61
  43.5 14.0 %all-to-all-done.1 = bf16[64,4,256]{2,1,0:T(4,128)(2,1)S(1)} async-done(((bf16[64,4,256]{2,1,0:T(4,128)(2,1)}), bf16[64,4,256]{2,1,0:T(4,128)(2,1)S(1)}, u32[]{:S(2)}, u32[]{:S(2)}) %all-to-all-start.1) | async-done | bytes 131104 | tf_op jit(solution)/shard_map/all_to_all | solution.py:48
  57.6 2.5 %fusion.9 = f32[64,4,256]{2,0,1:T(8,128)S(1)} fusion(bf16[64,4,2048]{2,1,0:T(4,128)(2,1)S(1)} %mul.61, bf16[256,256]{1,0:T(8,128)(2,1)S(1)} %reshape.154, bf16[2048,256]{1,0:T(8,128)(2,1)} %param.6, bf16[32,8,16,128]{3,2,1,0:T(8,128)(2,1)S(1)} %bitcast.41), kind=kOutput, calls=%fused_computation.16 | convolution fusion | flops 538443776 | bytes 3538944 | tf_op jit(solution)/shard_map/okp,pf->okf/dot_general | solution.py:59
  60.1 0.9 copy.56
  61.0 5.0 %all-to-all-start.2 = ((f32[64,4,256]{2,1,0:T(4,128)}), f32[64,4,256]{2,1,0:T(4,128)S(1)}, u32[]{:S(2)}, u32[]{:S(2)}) async-start(f32[64,4,256]{2,1,0:T(4,128)} %copy.56), calls=%async_computation.2 | async-start | bytes 524288 | tf_op jit(solution)/shard_map/all_to_all | solution.py:65
  66.4 17.5 %all-to-all-done.2 = f32[64,4,256]{2,1,0:T(4,128)S(1)} async-done(((f32[64,4,256]{2,1,0:T(4,128)}), f32[64,4,256]{2,1,0:T(4,128)S(1)}, u32[]{:S(2)}, u32[]{:S(2)}) %all-to-all-start.2) | async-done | bytes 262176 | tf_op jit(solution)/shard_map/all_to_all | solution.py:65
  84.0 0.2 fusion.5
  84.3 0.2 convolution_convert_fusion
  84.6 22.3 %all_to_all.38 = bf16[64,4,256]{2,1,0:T(4,128)(2,1)S(1)} all-to-all(bf16[64,4,256]{2,1,0:T(4,128)(2,1)S(1)} %copy.57), channel_id=1, replica_groups=mesh['pix'=64,'tm'=8] {'pix'}, dimensions={0} | all-to-all | bytes 262144 | tf_op jit(solution)/shard_map/all_to_all | solution.py:48
  107.3 0.5 slice.21
  108.6 0.6 fusion.1
  109.3 0.8 select_reduce_fusion
  110.1 14.2 %all_to_all.39 = f32[8,33,128]{2,1,0:T(8,128)S(1)} all-to-all(f32[8,33,128]{2,1,0:T(8,128)S(1)} %maximum_maximum_fusion), channel_id=1, replica_groups=mesh['pix'=64,'tm'=8] {'tm'}, dimensions={0} | all-to-all | bytes 270336 | tf_op jit(solution)/shard_map/all_to_all | solution.py:100
  124.3 0.6 slice.27
  125.8 8.5 %all_to_all.40 = f32[8,32,128]{2,1,0:T(8,128)S(1)} all-to-all(f32[8,32,128]{2,1,0:T(8,128)S(1)} %broadcast_in_dim.30), channel_id=1, replica_groups=mesh['pix'=64,'tm'=8] {'tm'}, dimensions={0} | all-to-all | bytes 262144 | tf_op jit(solution)/shard_map/all_to_all | solution.py:109
  134.3 0.7 copy.80
  (38 shorter events, 2.1 us)
Async XLA Ops:
  0.6 41.8 %copy-start.2 = (s32[256]{0:T(256)S(1)}, s32[256]{0:T(256)}, u32[]{:S(2)}) copy-start(s32[256]{0:T(256)} %param.9) | copy-start | bytes 3076
  37.8 19.8 %all-to-all-start.1 = ((bf16[64,4,256]{2,1,0:T(4,128)(2,1)}), bf16[64,4,256]{2,1,0:T(4,128)(2,1)S(1)}, u32[]{:S(2)}, u32[]{:S(2)}) async-start(bf16[64,4,256]{2,1,0:T(4,128)(2,1)} %copy.54), calls=%async_computation.1 | async-start | bytes 262144 | tf_op jit(solution)/shard_map/all_to_all | solution.py:48
  60.1 23.9 %copy-start = (bf16[32,256]{1,0:T(8,128)(2,1)S(1)}, bf16[32,256]{1,0:T(8,128)(2,1)}, u32[]{:S(2)}) copy-start(bf16[32,256]{1,0:T(8,128)(2,1)} %param.7) | copy-start | bytes 49156
  61.0 22.9 %all-to-all-start.2 = ((f32[64,4,256]{2,1,0:T(4,128)}), f32[64,4,256]{2,1,0:T(4,128)S(1)}, u32[]{:S(2)}, u32[]{:S(2)}) async-start(f32[64,4,256]{2,1,0:T(4,128)} %copy.56), calls=%async_computation.2 | async-start | bytes 524288 | tf_op jit(solution)/shard_map/all_to_all | solution.py:65
  66.0 42.5 %copy-start.3 = (bf16[2048,256]{1,0:T(8,128)(2,1)S(1)}, bf16[2048,256]{1,0:T(8,128)(2,1)}, u32[]{:S(2)}) copy-start(bf16[2048,256]{1,0:T(8,128)(2,1)} %param.6) | copy-start | bytes 3145732
  84.3 24.9 %copy-start.1 = (bf16[32,256]{1,0:T(8,128)(2,1)}, bf16[32,256]{1,0:T(8,128)(2,1)S(1)}, u32[]{:S(2)}) copy-start(bf16[32,256]{1,0:T(8,128)(2,1)S(1)} %fusion.5) | copy-start | bytes 49156

commit v8 on v4

--- a/solution.py
+++ b/solution.py
@@ -1,9 +1,38 @@
 import jax
 import jax.numpy as jnp
 from jax import lax
+from jax.experimental import pallas as pl
+from jax.experimental.pallas import tpu as pltpu
 from jax.sharding import PartitionSpec as P
 
 BLOCK = 128
+CHUNK = 256
+
+
+def first_pass_kernel(map_t_ref, map_ref, traces_ref, movie_ref, out_ref):
+    acc = jnp.zeros(out_ref.shape, jnp.float32)
+    for c in range(movie_ref.shape[0] // CHUNK):
+        rows = pl.ds(c * CHUNK, CHUNK)
+        rebuilt = jnp.dot(map_t_ref[rows, :], traces_ref[...], preferred_element_type=jnp.float32)
+        residual = (movie_ref[rows, :].astype(jnp.float32) - rebuilt).astype(jnp.bfloat16)
+        acc = acc + jnp.dot(map_ref[:, rows], residual, preferred_element_type=jnp.float32)
+    out_ref[...] = acc
+
+
+def first_pass(dense_map, slot_traces, movie):
+    slots, pixels = dense_map.shape
+    frames = movie.shape[1]
+    return pl.pallas_call(
+        first_pass_kernel,
+        out_shape=jax.ShapeDtypeStruct((slots, frames), jnp.float32),
+        in_specs=[pl.BlockSpec(memory_space=pltpu.VMEM)] * 4,
+        out_specs=pl.BlockSpec(memory_space=pltpu.VMEM),
+        cost_estimate=pl.CostEstimate(
+            flops=4 * slots * pixels * frames,
+            bytes_accessed=2 * (2 * slots * pixels + slots * frames + pixels * frames) + 4 * slots * frames,
+            transcendentals=0,
+        ),
+    )(dense_map.T, dense_map, slot_traces, movie)
 
 
 def local(movie, traces, footprints, slot_block, slot_neuron, bucket_fill):
@@ -55,13 +84,7 @@
         return (movie.astype(jnp.float32) - rebuilt).astype(jnp.bfloat16)
 
     slot_traces = slot_rows(traces)
-    residual = residual_of(slot_traces)
-    projection = jnp.einsum(
-        "okp,pf->okf",
-        dense_map.reshape(pix_count, capacity, block_count * BLOCK),
-        residual,
-        preferred_element_type=jnp.float32,
-    )
+    projection = first_pass(dense_map, slot_traces, movie).reshape(pix_count, capacity, frames)
     got_proj = lax.all_to_all(
         projection, "pix", split_axis=0, concat_axis=0, tiled=True
     ).reshape(slot_total, frames)

time: 133 us -> 136 us (1.023)
  Pallas kernels: 0 us -> 3.58 us
  local copies, waits for them, and re-layouts: 3.2 us -> 6.07 us
  matrix products: 5.42 us -> 2.87 us
    pallas_call x0 -> x1, Pallas kernels: none -> 3.58 us  [first_pass(): pl.pallas_call(first_pass_kernel, out_shape=jax.ShapeDtypeStruct((slots,...]
    dot_general x1 -> x0, matrix products: 2.55 us -> none  [local(): jnp.einsum('okp,pf->okf', dense_map.reshape(pix_count, capacity, block_co...]
    reshape x0 -> x1, local copies, waits for them, and re-layouts: none -> 1.73 us  [local(): first_pass(dense_map, slot_traces, movie)]
    all_to_all x1, waiting for transfers between devices: 14 us -> 12.6 us  [slot_rows(): got = lax.all_to_all(picked, 'pix', split_axis=0, concat_axis=0, tiled=True)]
  transfers between devices with their start and end apart: 2 -> 2, of which waited for: 2 -> 2; matrix products, arithmetic and copies ran while one was open for 1% -> 2% of each run, Pallas kernels for 0% -> 0%
where the time goes in v8:
time: 136 us; the launch traced here: 135 us
  blocking collectives  77.5 us (57%)
  waiting for transfers between devices  30.2 us (22%)
  starting transfers between devices  9.66 us (7%)
  local copies, waits for them, and re-layouts  6.07 us (4%)
  other arithmetic  4.24 us (3%)
  Pallas kernels  3.58 us (3%)
  matrix products  2.87 us (2%)
    all_to_all x1, blocking collectives, local(): lax.all_to_all(jnp.concatenate([slot_neuron.reshape(pix_count, capacity)....  32.4 us
    all_to_all x1, blocking collectives, slot_rows(): got = lax.all_to_all(picked, 'pix', split_axis=0, concat_axis=0, tiled=True)  22.3 us
    all_to_all x1, waiting for transfers between devices, local(): lax.all_to_all(projection, 'pix', split_axis=0, concat_axis=0, tiled=True)  17.5 us
    all_to_all x1, blocking collectives, local(): lax.all_to_all(stacked.reshape(tm_count, chunk, BLOCK), 'tm', split_axis=...  14 us
    all_to_all x1, waiting for transfers between devices, slot_rows(): got = lax.all_to_all(picked, 'pix', split_axis=0, concat_axis=0, tiled=True)  12.6 us
    all_to_all x1, blocking collectives, local(): lax.all_to_all(jnp.broadcast_to(mine, (tm_count, chunk, BLOCK)), 'tm', sp...  8.85 us
    all_to_all x1, starting transfers between devices, local(): lax.all_to_all(projection, 'pix', split_axis=0, concat_axis=0, tiled=True)  5.04 us
    all_to_all x1, starting transfers between devices, slot_rows(): got = lax.all_to_all(picked, 'pix', split_axis=0, concat_axis=0, tiled=True)  4.62 us
  transfers between devices with their start and end apart: 2, of which 2 were waited for; matrix products, arithmetic and copies ran while one was open for 2% of the time, Pallas kernels for 0%

profile of v8, /device:TPU:1, one launch (start us, length us, event | category | flops | bytes accessed | tf_op | source)
XLA Modules:
  0.0 135.0 jit_solution(12450188866403083428)
XLA Ops:
  0.6 0.7 convert_element_type.56
  1.3 0.7 iota_compare_fusion.4
  2.3 1.0 fusion.5
  3.5 32.4 %all_to_all.37 = f32[64,1,8]{2,1,0:T(1,128)S(1)} all-to-all(f32[64,1,8]{2,1,0:T(1,128)S(1)} %bitcast.37), channel_id=1, replica_groups=mesh['pix'=64,'tm'=8] {'pix'}, dimensions={0} | all-to-all | bytes 4096 | tf_op jit(solution)/shard_map/all_to_all | solution.py:57
  36.0 1.0 convolution_convert_fusion.1
  37.0 0.8 copy.37
  37.8 4.6 %all-to-all-start.1 = ((bf16[64,4,256]{2,1,0:T(4,128)(2,1)}), bf16[64,4,256]{2,1,0:T(4,128)(2,1)S(1)}, u32[]{:S(2)}, u32[]{:S(2)}) async-start(bf16[64,4,256]{2,1,0:T(4,128)(2,1)} %copy.37), calls=%async_computation.1 | async-start | bytes 262144 | tf_op jit(solution)/shard_map/all_to_all | solution.py:77
  42.5 0.7 broadcast_multiply_fusion
  43.2 0.3 copy.48
  43.5 1.4 %copy.38.map_t_ref = bf16[2048,256]{1,0:T(8,128)(2,1)} copy(bf16[2048,256]{0,1:T(8,128)(2,1)S(1)} %bitcast.32) | data formatting | bytes 2097152 | tf_op jit(solution)/shard_map/transpose | solution.py:35
  44.9 12.6 %all-to-all-done.1 = bf16[64,4,256]{2,1,0:T(4,128)(2,1)S(1)} async-done(((bf16[64,4,256]{2,1,0:T(4,128)(2,1)}), bf16[64,4,256]{2,1,0:T(4,128)(2,1)S(1)}, u32[]{:S(2)}, u32[]{:S(2)}) %all-to-all-start.1) | async-done | bytes 131104 | tf_op jit(solution)/shard_map/all_to_all | solution.py:77
  57.5 0.7 reshape.148.traces_ref
  58.2 3.6 %shard_map.77 = f32[256,256]{1,0:T(8,128)} custom-call(bf16[2048,256]{1,0:T(8,128)(2,1)} %copy.38.map_t_ref, bf16[256,2048]{1,0:T(8,128)(2,1)} %bitcast.33, bf16[256,256]{1,0:T(8,128)(2,1)} %reshape.148.traces_ref, bf16[2048,256]{1,0:T(8,128)(2,1)} %movie_ref.1), custom_call_target="tpu_custom_call" | custom-call | flops 536870912 | bytes 3538944 | tf_op jit(solution)/shard_map/pallas_call | solution.py:25
  61.8 1.7 %reshape.149 = f32[64,4,256]{2,1,0:T(4,128)} reshape(f32[256,256]{1,0:T(8,128)} %shard_map.77) | data formatting | bytes 524288 | tf_op jit(solution)/shard_map/reshape | solution.py:87
  63.5 5.0 %all-to-all-start.2 = ((f32[64,4,256]{2,1,0:T(4,128)}), f32[64,4,256]{2,1,0:T(4,128)S(1)}, u32[]{:S(2)}, u32[]{:S(2)}) async-start(f32[64,4,256]{2,1,0:T(4,128)} %reshape.149), calls=%async_computation.2 | async-start | bytes 524288 | tf_op jit(solution)/shard_map/all_to_all | solution.py:88
  68.9 17.5 %all-to-all-done.2 = f32[64,4,256]{2,1,0:T(4,128)S(1)} async-done(((f32[64,4,256]{2,1,0:T(4,128)}), f32[64,4,256]{2,1,0:T(4,128)S(1)}, u32[]{:S(2)}, u32[]{:S(2)}) %all-to-all-start.2) | async-done | bytes 262176 | tf_op jit(solution)/shard_map/all_to_all | solution.py:88
  86.6 0.2 fusion.3
  86.8 0.2 convolution_convert_fusion
  87.2 22.3 %all_to_all.38 = bf16[64,4,256]{2,1,0:T(4,128)(2,1)S(1)} all-to-all(bf16[64,4,256]{2,1,0:T(4,128)(2,1)S(1)} %copy.39), channel_id=1, replica_groups=mesh['pix'=64,'tm'=8] {'pix'}, dimensions={0} | all-to-all | bytes 262144 | tf_op jit(solution)/shard_map/all_to_all | solution.py:77
  109.9 0.6 fusion
  110.5 0.8 select_reduce_fusion
  111.3 14.0 %all_to_all.39 = f32[8,33,128]{2,1,0:T(8,128)S(1)} all-to-all(f32[8,33,128]{2,1,0:T(8,128)S(1)} %reshape.154), channel_id=1, replica_groups=mesh['pix'=64,'tm'=8] {'tm'}, dimensions={0} | all-to-all | bytes 270336 | tf_op jit(solution)/shard_map/all_to_all | solution.py:111
  125.3 8.8 %all_to_all.40 = f32[8,33,128]{2,1,0:T(8,128)S(1)} all-to-all(f32[8,33,128]{2,1,0:T(8,128)S(1)} %broadcast_in_dim.23), channel_id=1, replica_groups=mesh['pix'=64,'tm'=8] {'tm'}, dimensions={0} | all-to-all | bytes 270336 | tf_op jit(solution)/shard_map/all_to_all | solution.py:115
  134.2 0.8 fusion.7
  (35 shorter events, 1.7 us)
Async XLA Ops:
  0.6 41.8 %copy-start.4 = (s32[256]{0:T(256)S(1)}, s32[256]{0:T(256)}, u32[]{:S(2)}) copy-start(s32[256]{0:T(256)} %param.9) | copy-start | bytes 3076
  37.8 19.8 %all-to-all-start.1 = ((bf16[64,4,256]{2,1,0:T(4,128)(2,1)}), bf16[64,4,256]{2,1,0:T(4,128)(2,1)S(1)}, u32[]{:S(2)}, u32[]{:S(2)}) async-start(bf16[64,4,256]{2,1,0:T(4,128)(2,1)} %copy.37), calls=%async_computation.1 | async-start | bytes 262144 | tf_op jit(solution)/shard_map/all_to_all | solution.py:77
  43.5 1.4 %copy-start = (bf16[32,8,16,128]{3,1,2,0:T(8,128)(2,1)}, bf16[32,8,16,128]{3,1,2,0:T(8,128)(2,1)S(1)}, u32[]{:S(2)}) copy-start(bf16[32,8,16,128]{3,1,2,0:T(8,128)(2,1)S(1)} %copy.48) | copy-start | bytes 3145732
  61.8 24.8 %copy-start.2 = (bf16[32,256]{1,0:T(8,128)(2,1)S(1)}, bf16[32,256]{1,0:T(8,128)(2,1)}, u32[]{:S(2)}) copy-start(bf16[32,256]{1,0:T(8,128)(2,1)} %param.7) | copy-start | bytes 49156
  63.5 22.9 %all-to-all-start.2 = ((f32[64,4,256]{2,1,0:T(4,128)}), f32[64,4,256]{2,1,0:T(4,128)S(1)}, u32[]{:S(2)}, u32[]{:S(2)}) async-start(f32[64,4,256]{2,1,0:T(4,128)} %reshape.149), calls=%async_computation.2 | async-start | bytes 524288 | tf_op jit(solution)/shard_map/all_to_all | solution.py:88
  68.6 41.3 %copy-start.1 = (bf16[2048,256]{1,0:T(8,128)(2,1)S(1)}, bf16[2048,256]{1,0:T(8,128)(2,1)}, u32[]{:S(2)}) copy-start(bf16[2048,256]{1,0:T(8,128)(2,1)} %movie_ref.1) | copy-start | bytes 3145732
  86.8 23.7 %copy-start.3 = (bf16[32,256]{1,0:T(8,128)(2,1)}, bf16[32,256]{1,0:T(8,128)(2,1)S(1)}, u32[]{:S(2)}) copy-start(bf16[32,256]{1,0:T(8,128)(2,1)S(1)} %fusion.3) | copy-start | bytes 49156

commit v9 on v4

--- a/solution.py
+++ b/solution.py
@@ -25,21 +25,13 @@
     dense_map = (block_pick.astype(jnp.bfloat16)[:, :, None] * masked[:, None, :]).reshape(
         slot_total, block_count * BLOCK
     )
-    asked_and_power = lax.all_to_all(
-        jnp.concatenate(
-            [slot_neuron.reshape(pix_count, capacity).astype(jnp.float32), power_op], axis=1
-        ),
-        "pix",
-        split_axis=0,
-        concat_axis=0,
-        tiled=True,
+    asked = lax.all_to_all(
+        slot_neuron.reshape(pix_count, capacity), "pix", split_axis=0, concat_axis=0, tiled=True
     )
-    asked = asked_and_power[:, :capacity].astype(jnp.int32)
     asked_flat = asked.reshape(slot_total)
     row_pick = (asked[:, :, None] == jnp.arange(neur_local, dtype=jnp.int32)[None, None, :]).astype(
         jnp.bfloat16
     )
-    got_power = asked_and_power[:, capacity:].reshape(slot_total)
 
     def slot_rows(source_rows):
         picked = jnp.einsum(
@@ -62,9 +54,15 @@
         residual,
         preferred_element_type=jnp.float32,
     )
-    got_proj = lax.all_to_all(
-        projection, "pix", split_axis=0, concat_axis=0, tiled=True
-    ).reshape(slot_total, frames)
+    got = lax.all_to_all(
+        jnp.concatenate([projection.reshape(pix_count, capacity * frames), power_op], axis=1),
+        "pix",
+        split_axis=0,
+        concat_axis=0,
+        tiled=True,
+    )
+    got_proj = got[:, : capacity * frames].reshape(slot_total, frames)
+    got_power = got[:, capacity * frames :].reshape(slot_total)
     owner_pick = (jnp.arange(neur_local, dtype=jnp.int32)[:, None] == asked_flat[None, :]).astype(
         jnp.float32
     )

time: 133 us -> 134 us (level)
  blocking collectives: 77.7 us -> 45.9 us
  starting transfers between devices: 9.66 us -> 28.8 us
  waiting for transfers between devices: 31.5 us -> 42.1 us
  local copies, waits for them, and re-layouts: 3.2 us -> 5.2 us
    all_to_all x1 -> x0, blocking collectives: 32.4 us -> none  [local(): lax.all_to_all(jnp.concatenate([slot_neuron.reshape(pix_count, capacity)....]
    all_to_all x1 -> x2, starting transfers between devices: 5.04 us -> 24.1 us  [the longest x1 19.1 us: local(): lax.all_to_all(slot_neuron.reshape(pix_count, capacity), 'pix', split_axi...]
    all_to_all x1 -> x2, waiting for transfers between devices: 17.5 us -> 30 us  [the longest x1 17.3 us: local(): lax.all_to_all(jnp.concatenate([projection.reshape(pix_count, capacity *...]
    all_to_all x0 -> x3, local copies, waits for them, and re-layouts: none -> 2.92 us  [the longest x2 1.91 us: local(): lax.all_to_all(slot_neuron.reshape(pix_count, capacity), 'pix', split_axi...]
    all_to_all x1, waiting for transfers between devices: 14 us -> 12 us  [slot_rows(): got = lax.all_to_all(picked, 'pix', split_axis=0, concat_axis=0, tiled=True)]
  transfers between devices with their start and end apart: 2 -> 3, of which waited for: 2 -> 3; matrix products, arithmetic and copies ran while one was open for 1% -> 4% of each run, Pallas kernels for 0% -> 0%
where the time goes in v9:
time: 134 us; the launch traced here: 133 us
  blocking collectives  45.9 us (34%)
  waiting for transfers between devices  42.1 us (31%)
  starting transfers between devices  28.8 us (21%)
  matrix products  5.44 us (4%)
  local copies, waits for them, and re-layouts  5.2 us (4%)
  other arithmetic  4.84 us (4%)
    all_to_all x1, blocking collectives, slot_rows(): got = lax.all_to_all(picked, 'pix', split_axis=0, concat_axis=0, tiled=True)  22.9 us
    all_to_all x1, starting transfers between devices, local(): lax.all_to_all(slot_neuron.reshape(pix_count, capacity), 'pix', split_axi...  19.1 us
    all_to_all x1, waiting for transfers between devices, local(): lax.all_to_all(jnp.concatenate([projection.reshape(pix_count, capacity *...  17.3 us
    all_to_all x1, blocking collectives, local(): lax.all_to_all(stacked.reshape(tm_count, chunk, BLOCK), 'tm', split_axis=...  14.2 us
    all_to_all x1, waiting for transfers between devices, local(): lax.all_to_all(slot_neuron.reshape(pix_count, capacity), 'pix', split_axi...  12.7 us
    all_to_all x1, waiting for transfers between devices, slot_rows(): got = lax.all_to_all(picked, 'pix', split_axis=0, concat_axis=0, tiled=True)  12 us
    all_to_all x1, blocking collectives, local(): lax.all_to_all(jnp.broadcast_to(mine, (tm_count, chunk, BLOCK)), 'tm', sp...  8.85 us
    all_to_all x1, starting transfers between devices, local(): lax.all_to_all(jnp.concatenate([projection.reshape(pix_count, capacity *...  5.04 us
  transfers between devices with their start and end apart: 3, of which 3 were waited for; matrix products, arithmetic and copies ran while one was open for 4% of the time, Pallas kernels for 0%

profile of v9, /device:TPU:1, one launch (start us, length us, event | category | flops | bytes accessed | tf_op | source)
XLA Modules:
  0.0 133.1 jit_solution(4773587683293652394)
XLA Ops:
  0.6 1.4 %all_to_all.26 = s32[64,1,4]{2,0,1:T(8,128)} reshape(s32[256]{0:T(256)} %param.10) | data formatting | bytes 2048 | tf_op jit(solution)/shard_map/all_to_all | solution.py:28
  2.0 19.1 %all-to-all-start = ((s32[64,1,4]{2,1,0:T(1,128)}), s32[64,1,4]{2,1,0:T(1,128)S(1)}, u32[]{:S(2)}, u32[]{:S(2)}) async-start(s32[64,1,4]{2,1,0:T(1,128)} %bitcast), calls=%async_computation | async-start | bytes 65536 | tf_op jit(solution)/shard_map/all_to_all | solution.py:28
  21.1 0.7 iota_compare_fusion.8
  21.8 12.7 %all-to-all-done = s32[64,1,4]{2,1,0:T(1,128)S(1)} async-done(((s32[64,1,4]{2,1,0:T(1,128)}), s32[64,1,4]{2,1,0:T(1,128)S(1)}, u32[]{:S(2)}, u32[]{:S(2)}) %all-to-all-start) | async-done | bytes 1056 | tf_op jit(solution)/shard_map/all_to_all | solution.py:28
  34.6 1.0 convolution_convert_fusion.1
  35.6 0.8 copy.28
  36.3 4.6 %all-to-all-start.1 = ((bf16[64,4,256]{2,1,0:T(4,128)(2,1)}), bf16[64,4,256]{2,1,0:T(4,128)(2,1)S(1)}, u32[]{:S(2)}, u32[]{:S(2)}) async-start(bf16[64,4,256]{2,1,0:T(4,128)(2,1)} %copy.28), calls=%async_computation.1 | async-start | bytes 262144 | tf_op jit(solution)/shard_map/all_to_all | solution.py:40
  41.0 0.7 iota_compare_fusion.4
  41.9 1.0 fusion.14
  43.1 0.7 broadcast_multiply_fusion
  43.8 0.3 mul.48
  44.1 12.0 %all-to-all-done.1 = bf16[64,4,256]{2,1,0:T(4,128)(2,1)S(1)} async-done(((bf16[64,4,256]{2,1,0:T(4,128)(2,1)}), bf16[64,4,256]{2,1,0:T(4,128)(2,1)S(1)}, u32[]{:S(2)}, u32[]{:S(2)}) %all-to-all-start.1) | async-done | bytes 131104 | tf_op jit(solution)/shard_map/all_to_all | solution.py:40
  56.1 2.6 %convolution_bitcast_fusion = f32[4,8,8,256]{3,2,1,0:T(8,128)S(1)} fusion(bf16[64,4,2048]{2,1,0:T(4,128)(2,1)S(1)} %mul.48, bf16[256,256]{1,0:T(8,128)(2,1)S(1)} %reshape.158, bf16[2048,256]{1,0:T(8,128)(2,1)} %param.6, bf16[32,8,16,128]{3,2,1,0:T(8,128)(2,1)S(1)} %bitcast.42), kind=kOutput, calls=%fused_computation.6 | convolution fusion | flops 538443776 | bytes 3538944 | tf_op jit(solution)/shard_map/okp,pf->okf/dot_general | solution.py:51
  58.8 1.0 copy.31
  59.8 5.0 %all-to-all-start.2 = ((f32[64,1,1028]{2,1,0:T(1,128)}), f32[64,1,1028]{2,1,0:T(1,128)S(1)}, u32[]{:S(2)}, u32[]{:S(2)}) async-start(f32[64,1,1028]{2,1,0:T(1,128)} %copy.31), calls=%async_computation.2 | async-start | bytes 589824 | tf_op jit(solution)/shard_map/all_to_all | solution.py:57
  64.8 0.5 broadcast.77
  65.3 0.7 reduce.5
  66.2 17.3 %all-to-all-done.2 = f32[64,1,1028]{2,1,0:T(1,128)S(1)} async-done(((f32[64,1,1028]{2,1,0:T(1,128)}), f32[64,1,1028]{2,1,0:T(1,128)S(1)}, u32[]{:S(2)}, u32[]{:S(2)}) %all-to-all-start.2) | async-done | bytes 263200 | tf_op jit(solution)/shard_map/all_to_all | solution.py:57
  84.5 22.9 %all_to_all.41 = bf16[64,4,256]{2,1,0:T(4,128)(2,1)S(1)} all-to-all(bf16[64,4,256]{2,1,0:T(4,128)(2,1)S(1)} %copy.32), channel_id=1, replica_groups=mesh['pix'=64,'tm'=8] {'pix'}, dimensions={0} | all-to-all | bytes 262144 | tf_op jit(solution)/shard_map/all_to_all | solution.py:40
  107.8 0.6 fusion.1
  108.4 0.8 select_reduce_fusion
  109.2 14.2 %all_to_all.42 = f32[8,33,128]{2,1,0:T(8,128)S(1)} all-to-all(f32[8,33,128]{2,1,0:T(8,128)S(1)} %reshape.164), channel_id=1, replica_groups=mesh['pix'=64,'tm'=8] {'tm'}, dimensions={0} | all-to-all | bytes 270336 | tf_op jit(solution)/shard_map/all_to_all | solution.py:86
  123.5 8.8 %all_to_all.43 = f32[8,33,128]{2,1,0:T(8,128)S(1)} all-to-all(f32[8,33,128]{2,1,0:T(8,128)S(1)} %broadcast_in_dim.23), channel_id=1, replica_groups=mesh['pix'=64,'tm'=8] {'tm'}, dimensions={0} | all-to-all | bytes 270336 | tf_op jit(solution)/shard_map/all_to_all | solution.py:90
  132.3 0.8 fusion.16
  (35 shorter events, 2.0 us)
Async XLA Ops:
  2.0 32.5 %all-to-all-start = ((s32[64,1,4]{2,1,0:T(1,128)}), s32[64,1,4]{2,1,0:T(1,128)S(1)}, u32[]{:S(2)}, u32[]{:S(2)}) async-start(s32[64,1,4]{2,1,0:T(1,128)} %bitcast), calls=%async_computation | async-start | bytes 65536 | tf_op jit(solution)/shard_map/all_to_all | solution.py:28
  36.3 19.8 %all-to-all-start.1 = ((bf16[64,4,256]{2,1,0:T(4,128)(2,1)}), bf16[64,4,256]{2,1,0:T(4,128)(2,1)S(1)}, u32[]{:S(2)}, u32[]{:S(2)}) async-start(bf16[64,4,256]{2,1,0:T(4,128)(2,1)} %copy.28), calls=%async_computation.1 | async-start | bytes 262144 | tf_op jit(solution)/shard_map/all_to_all | solution.py:40
  59.8 23.7 %all-to-all-start.2 = ((f32[64,1,1028]{2,1,0:T(1,128)}), f32[64,1,1028]{2,1,0:T(1,128)S(1)}, u32[]{:S(2)}, u32[]{:S(2)}) async-start(f32[64,1,1028]{2,1,0:T(1,128)} %copy.31), calls=%async_computation.2 | async-start | bytes 589824 | tf_op jit(solution)/shard_map/all_to_all | solution.py:57
  64.8 19.1 %copy-start = (bf16[32,256]{1,0:T(8,128)(2,1)S(1)}, bf16[32,256]{1,0:T(8,128)(2,1)}, u32[]{:S(2)}) copy-start(bf16[32,256]{1,0:T(8,128)(2,1)} %param.7) | copy-start | bytes 49156
  83.6 24.2 %copy-start.2 = (bf16[2048,256]{1,0:T(8,128)(2,1)S(1)}, bf16[2048,256]{1,0:T(8,128)(2,1)}, u32[]{:S(2)}) copy-start(bf16[2048,256]{1,0:T(8,128)(2,1)} %param.6) | copy-start | bytes 3145732
  84.2 24.2 %copy-start.1 = (bf16[32,256]{1,0:T(8,128)(2,1)}, bf16[32,256]{1,0:T(8,128)(2,1)S(1)}, u32[]{:S(2)}) copy-start(bf16[32,256]{1,0:T(8,128)(2,1)S(1)} %fusion.5) | copy-start | bytes 49156
